TPU v7x, 512 devices: a whole 4x4x16 slice. The times are simulated.
512 devices in a mesh: pipe: 16 (over z_hi, y), zero: 32 (over z_lo, x, core).
Axes of the slice: x: 4, y: 4, z: 16 (z_hi: 4, z_lo: 4; z = z_hi * 4 + z_lo), core: 2. Of those that a mesh axis runs over, the one named last changes fastest.
Arguments:
- residual: bfloat16 [16, 2048, 4096], P('pipe', 'zero'), may hold values from -6 to 6
- norm_gain: bfloat16 [16, 4096], P('pipe'), may hold values from 0.099609375 to 1.8984375
- queries: bfloat16 [16, 2048, 4096], P('pipe', 'zero'), may hold values from -74 to 74
- cached_kv: bfloat16 [16, 512, 1024], P('pipe', 'zero'), may hold values from -6 to 6
- panel_blocks: bfloat16 [16, 160, 128, 128], P('pipe', 'zero'), may hold values from -0.125 to 0.125
- block_rows: int32 [16, 8, 20], P('pipe'), may hold values from 0 to 31, as said below
- counts: int32 [16, 8], P('pipe'), may hold values from 12 to 20, as said below
Outputs:
- passed: bfloat16 [16, 2048, 4096], P('pipe', 'zero')
- new_kv: bfloat16 [16, 2048, 1024], P('pipe', 'zero')
Inputs may be any that keep to these rules, and one draw needn't show every extreme that they name: `block_rows`: row blocks named by the slots of one panel are all different. `counts`: slots at or beyond a panel's count are padding.
All inputs are finite; a program needn't handle non-finite values.
Results may differ from a plain program's by a relative error of at most 0.0047.
The roundings to bfloat16 on the way count: a program that leaves them out, or rounds other values in their place, can miss the bound.
Values may be sent and summed in bfloat16 or wider, within the bound.
No kernel may reach another device: no remote copies, remote signals or barrier semaphores. Data moves between devices by JAX's collectives and lax.ppermute only.
A program may use at most 64 MiB of HBM per device.

v0:
```python
import math

import jax
import jax.numpy as jnp
from jax import lax
from jax.sharding import PartitionSpec as P

QH = 32
KVH = 4
HD = 128


def passed_along(block, axis, distance):
    devices = range(lax.axis_size(axis))
    route = [((i - distance) % len(devices), i) for i in devices]
    return lax.ppermute(block, axis, route)


def local(residual, norm_gain, queries, cached_kv, panel_blocks, block_rows, counts):
    row_count = residual.shape[1]
    model_width = residual.shape[2]
    zero_index = lax.axis_index("zero")
    stream = residual[0].astype(jnp.float32)
    normed = (
        stream
        * lax.rsqrt(jnp.mean(stream * stream, axis=-1, keepdims=True) + 1e-05)
        * norm_gain[0].astype(jnp.float32)
    ).astype(jnp.bfloat16)
    block_size = panel_blocks.shape[-1]
    panels = block_rows.shape[1]
    slot_depth = block_rows.shape[2]
    row_table = block_rows[0].reshape(-1)
    slot_live = (
        (jnp.arange(slot_depth)[None, :] < counts[0][:, None]).astype(jnp.float32).reshape(-1)
    )
    normed_grid = normed.reshape(row_count, model_width // block_size, block_size)
    kv_heads = KVH
    head_size = HD
    group_size = QH // KVH
    kv_width = kv_heads * head_size
    score_scale = 1.0 / math.sqrt(head_size)
    query_grid = queries[0].reshape(row_count, kv_heads, group_size, head_size)
    first_query = zero_index * row_count
    query_pos = first_query + jnp.arange(row_count)
    initial = (
        jnp.full((kv_heads, row_count, group_size), -1e30, jnp.float32),
        jnp.zeros((kv_heads, row_count, group_size), jnp.float32),
        jnp.zeros((kv_heads, row_count, group_size, head_size), jnp.float32),
    )

    def absorb(running, portion, visible):
        run_max, run_sum, run_acc = running
        key_count = portion.shape[0]
        key_grid = portion[:, :kv_width].reshape(key_count, kv_heads, head_size)
        value_grid = portion[:, kv_width:].reshape(key_count, kv_heads, head_size)
        scores = (
            jnp.einsum("rgjd,ngd->grjn", query_grid, key_grid, preferred_element_type=jnp.float32)
            * score_scale
        )
        visible_mask = visible[None, :, None, :]
        new_max = jnp.maximum(run_max, jnp.max(jnp.where(visible_mask, scores, -1e30), axis=-1))
        shrink = jnp.exp(run_max - new_max)
        weights = jnp.where(visible_mask, jnp.exp(scores - new_max[..., None]), 0.0)
        new_sum = run_sum * shrink + jnp.sum(weights, axis=-1)
        new_acc = run_acc * shrink[..., None] + jnp.einsum(
            "grjn,ngd->grjd",
            weights.astype(jnp.bfloat16),
            value_grid,
            preferred_element_type=jnp.float32,
        )
        return (new_max, new_sum, new_acc)

    chosen = jnp.take(normed_grid, row_table, axis=1)
    slot_terms = jnp.einsum(
        "rsk,skn->rsn",
        chosen,
        lax.all_gather(panel_blocks[0], "zero", axis=0, tiled=True),
        preferred_element_type=jnp.float32,
    )
    slot_terms = slot_terms * slot_live[None, :, None]
    summed = slot_terms.reshape(row_count, panels, slot_depth, block_size).sum(axis=2)
    kv_new = summed.reshape(row_count, panels * block_size).astype(jnp.bfloat16)
    cache_portion = lax.all_gather(cached_kv[0], "zero", axis=0, tiled=True)
    softmax_state = absorb(
        initial, cache_portion, jnp.ones((row_count, cache_portion.shape[0]), bool)
    )
    portion = lax.all_gather(kv_new, "zero", axis=0, tiled=True)
    key_pos = jnp.arange(portion.shape[0])
    visible = key_pos[None, :] <= query_pos[:, None]
    softmax_state = lax.cond(
        jnp.int32(0) <= first_query + row_count - 1,
        lambda state_in: absorb(state_in, portion, visible),
        lambda state_in: state_in,
        softmax_state,
    )
    run_max, denominator, run_acc = softmax_state
    attended = run_acc / denominator[..., None]
    attended = jnp.transpose(attended, (1, 0, 2, 3)).reshape(
        row_count, kv_heads * group_size * head_size
    )
    updated = (stream + attended).astype(jnp.bfloat16)
    passed = passed_along(updated[None], "pipe", 1)
    return (passed, kv_new[None])


def solution(mesh):
    in_specs = (
        P("pipe", "zero", None),
        P("pipe", None),
        P("pipe", "zero", None),
        P("pipe", "zero", None),
        P("pipe", "zero", None, None),
        P("pipe", None, None),
        P("pipe", None),
    )
    out_specs = (P("pipe", "zero", None), P("pipe", "zero", None))
    return jax.shard_map(local, mesh=mesh, in_specs=in_specs, out_specs=out_specs, check_vma=False)
```

profile of v0, /device:TPU:128, one launch (start us, length us, event | category | flops | bytes accessed | tf_op | source)
XLA Modules:
  0.0 305.9 jit_solution(14598807501692515659)
XLA Ops:
  7.2 0.0 copy-start
  7.2 0.0 all-gather.10.cloned.1.call-start
  7.2 0.7 all-gather.10.cloned.1.call-update
  7.9 0.0 all-gather.8.cloned.1.call-start
  8.0 0.7 all-gather.8.cloned.1.call-update
  8.7 0.0 all-gather.6.cloned.1.call-start
  8.7 1.1 convert_bitcast_fusion
  9.8 0.7 fusion.37
  10.6 0.8 reshape_squeeze.10
  11.3 0.8 reshape_squeeze.9
  12.1 0.1 reshape.131
  12.2 0.7 mul.79
  12.9 0.2 copy.67
  13.1 0.0 copy-done
  13.1 0.2 fusion.31
  13.4 0.7 fusion.34
  14.1 1.1 gather_fusion
  15.1 66.9 %all-gather.10.cloned.1.call-done = bf16[1,160,128,128]{3,2,0,1:T(8,128)(2,1)} async-done(((bf16[1,5,128,128]{3,2,0,1:T(8,128)(2,1)}), bf16[1,160,128,128]{3,2,0,1:T(8,128)(2,1)}) %all-gather.10.cloned.1.call-update) | async-done | bytes 5242896 | tf_op jit(solution)/shard_map/all_gather | solution.py:77
  82.0 6.4 %broadcast_multiply_fusion = f32[160,64,128]{2,1,0:T(8,128)} fusion(f32[160]{0:T(256)S(1)} %reshape.131, bf16[1,160,128,128]{3,2,0,1:T(8,128)(2,1)} %all-gather.10.cloned.1.call-done, bf16[160,64,128]{2,1,0:T(8,128)(2,1)S(1)} %gather_fusion, pred[160]{0:T(512)(128)(4,1)S(1)} %compare_and_fusion), kind=kOutput, calls=%fused_computation.24 | convolution fusion | flops 338165760 | bytes 13108000 | tf_op jit(solution)/shard_map/rsk,skn->rsn/dot_general | solution.py:74
  88.4 0.0 copy-start.2
  88.4 3.0 reduce_sum.38
  91.4 0.7 copy_bitcast_fusion
  92.1 0.0 all-gather.6.cloned.1.call-update
  92.1 0.0 copy-done.2
  92.1 0.1 copy.66
  92.2 55.0 %all-gather.8.cloned.1.call-done = bf16[1,512,1024]{2,1,0:T(8,128)(2,1)} async-done(((bf16[1,16,1024]{2,1,0:T(8,128)(2,1)}), bf16[1,512,1024]{2,1,0:T(8,128)(2,1)}) %all-gather.8.cloned.1.call-update) | async-done | bytes 1048592 | tf_op jit(solution)/shard_map/all_gather | solution.py:83
  147.2 1.5 copy.42
  148.8 0.1 fusion.42
  148.8 0.8 multiply_reduce_fusion
  149.6 1.3 fusion.15
  150.9 1.5 fusion.27
  152.4 64.2 %all-gather.6.cloned.1.call-done = bf16[2048,1024]{1,0:T(8,128)(2,1)} async-done(((bf16[64,1024]{1,0:T(8,128)(2,1)}), bf16[2048,1024]{1,0:T(8,128)(2,1)}) %all-gather.6.cloned.1.call-update) | async-done | bytes 4194320 | tf_op jit(solution)/shard_map/all_gather | solution.py:87
  216.7 26.3 %conditional.1 = ((f32[4,64,8]{2,1,0:T(8,128)S(1)}, f32[4,64,8,128]{3,2,1,0:T(8,128)S(1)})) conditional(s32[]{:T(128)} %convert_element_type.57, (f32[4,64,8]{2,1,0:T(8,128)S(1)}, f32[4,64,8,128]{3,2,1,0:T(8,128)S(1)}) %tuple.15, (s32[]{:T(128)}, s32[64,1]{0,1:T(1,128)S(1)}, s32[64,2048]{1,0:T(8,128)S(1)}, bf16[2048,1024]{1,0:T(8,128)(2,1)}, ...), branch_computations={%region_4.5_spmd, %region_5.8_spmd} | conditional | flops 2194280448 | bytes 75088664 | solution.py:90
  216.7 0.1 broadcast_compare_fusion
  216.8 6.5 %copy.49 = bf16[2048,1024]{0,1:T(8,128)(2,1)} copy(bf16[2048,1024]{1,0:T(8,128)(2,1)} %get-tuple-element.66) | data formatting | bytes 8388608 | tf_op jit(solution)/shard_map
  223.4 4.0 %fusion.41 = (bf16[2048,512]{0,1:T(8,128)(2,1)}, bf16[2048,512]{0,1:T(8,128)(2,1)S(1)}) fusion(bf16[2048,1024]{0,1:T(8,128)(2,1)} %copy.49), kind=kLoop, calls=%fused_computation.55 | loop fusion | bytes 8388608 | tf_op jit(solution)/shard_map/cond/branch_1_fun/slice | solution.py:55
  227.4 3.9 %select_reduce_fusion = (f32[4,64,8]{2,1,0:T(8,128)S(1)}, f32[4,64,8,2048]{3,2,1,0:T(8,128)S(1)}) fusion(pred[64,2048]{1,0:T(8,128)(4,1)S(1)} %broadcast_compare_fusion, bf16[2048,4,128,1]{0,2,3,1:T(8,128)(2,1)S(1)} %bitcast.62, bf16[64,4,8,128]{3,2,1,0:T(8,128)(2,1)S(1)} %get-tuple-element.67), kind=kOutput, calls=%fused_computation.2 | convolution fusion | flops 1086322688 | bytes 19537920 | tf_op jit(solution)/shard_map/cond/branch_1_fun/rgjd,ngd->grjn/dot_general | solution.py:57
  231.3 5.0 %fusion.1 = f32[4,64,8]{2,1,0:T(8,128)S(1)} fusion(f32[4,64,8,2048]{3,2,1,0:T(8,128)S(1)} %get-tuple-element.76, f32[4,64,8]{2,1,0:T(8,128)S(1)} %max.2, pred[64,2048]{1,0:T(8,128)(4,1)S(1)} %broadcast_compare_fusion), kind=kLoop, calls=%fused_computation.4 | loop fusion | flops 16775168 | bytes 16924672 | tf_op jit(solution)/shard_map/cond/branch_1_fun/reduce_sum | solution.py:64
  236.3 0.1 multiply_add_fusion
  236.4 6.5 %fusion.5 = f32[4,64,8,128]{3,2,1,0:T(8,128)S(1)} fusion(bf16[2048,4,128,1]{0,2,3,1:T(8,128)(2,1)} %bitcast.68, f32[4,64,8,2048]{3,2,1,0:T(8,128)S(1)} %get-tuple-element.76, f32[4,64,8]{2,1,0:T(8,128)S(1)} %max.2, pred[64,2048]{1,0:T(8,128)(4,1)S(1)} %broadcast_compare_fusion, f32[4,64,8,128]{3,2,1,0:T(8,128)S(1)} %get-tuple-element.32, ...), kind=kOutput, calls=%fused_computation.7 | convolution fusion | flops 1091043328 | bytes 21118976 | tf_op jit(solution)/shard_map/cond/branch_1_fun/grjn,ngd->grjd/dot_general | solution.py:65
  243.0 0.0 copy-start.1
  243.0 0.3 divide_bitcast_fusion
  243.3 0.1 copy.51
  243.5 0.2 reshape.128
  243.7 0.3 copy-done.1
  244.0 0.1 fusion.32
  244.1 3.3 %collective-permute-start = (bf16[1,64,4096]{2,1,0:T(8,128)(2,1)S(1)}, bf16[1,64,4096]{2,1,0:T(8,128)(2,1)S(1)}, u32[]{:S(2)}, u32[]{:S(2)}) collective-permute-start(bf16[1,64,4096]{2,1,0:T(8,128)(2,1)S(1)} %fusion.32), channel_id=1, source_target_pairs={{480,0},{0,32},{32,64},{64,96},{96,128},{128,160},{160,192},{192,2... | collective-permute-start | bytes 1572872 | tf_op jit(solution)/shard_map/ppermute | solution.py:16
  247.4 0.1 copy.48
  247.5 0.7 convert_element_type.67
  248.2 50.3 %collective-permute-done = bf16[1,64,4096]{2,1,0:T(8,128)(2,1)S(1)} collective-permute-done((bf16[1,64,4096]{2,1,0:T(8,128)(2,1)S(1)}, bf16[1,64,4096]{2,1,0:T(8,128)(2,1)S(1)}, u32[]{:S(2)}, u32[]{:S(2)}) %collective-permute-start) | collective-permute-done | bytes 524320 | tf_op jit(solution)/shard_map/ppermute | solution.py:16
  298.6 0.8 copy.87
  (10 shorter events, 0.1 us)
Async XLA Ops:
  7.2 6.0 %copy-start = (bf16[1,64,4096]{2,1,0:T(8,128)(2,1)S(1)}, bf16[1,64,4096]{2,1,0:T(8,128)(2,1)}, u32[]{:S(2)}) copy-start(bf16[1,64,4096]{2,1,0:T(8,128)(2,1)} %param.9) | copy-start | bytes 1572868
  7.2 74.8 %all-gather.10.cloned.1.call-start = ((), (), s32[]{:S(2)}) async-start(), calls=%async_computation.2 | async-start | bytes 5406720 | tf_op jit(solution)/shard_map/all_gather | solution.py:77
  7.9 139.3 %all-gather.8.cloned.1.call-start = ((), (), s32[]{:S(2)}) async-start(), calls=%async_computation.1 | async-start | bytes 1081344 | tf_op jit(solution)/shard_map/all_gather | solution.py:83
  8.7 208.0 %all-gather.6.cloned.1.call-start = ((), (), s32[]{:S(2)}) async-start(), calls=%async_computation | async-start | bytes 4325376 | tf_op jit(solution)/shard_map/all_gather | solution.py:87
  88.4 3.7 %copy-start.2 = (bf16[1,64,4096]{2,1,0:T(8,128)(2,1)S(1)}, bf16[1,64,4096]{2,1,0:T(8,128)(2,1)}, u32[]{:S(2)}) copy-start(bf16[1,64,4096]{2,1,0:T(8,128)(2,1)} %param.11) | copy-start | bytes 1572868
  243.0 1.0 copy-start.1
  244.1 54.5 %collective-permute-start = (bf16[1,64,4096]{2,1,0:T(8,128)(2,1)S(1)}, bf16[1,64,4096]{2,1,0:T(8,128)(2,1)S(1)}, u32[]{:S(2)}, u32[]{:S(2)}) collective-permute-start(bf16[1,64,4096]{2,1,0:T(8,128)(2,1)S(1)} %fusion.32), channel_id=1, source_target_pairs={{480,0},{0,32},{32,64},{64,96},{96,128},{128,160},{160,192},{192,2... | collective-permute-start | bytes 1572872 | tf_op jit(solution)/shard_map/ppermute | solution.py:16
Sparse Core Ops, SparseCore 0:
  10.1 71.8 all-gather.9
  84.2 63.0 all-gather.7
  150.0 66.6 all-gather.5
where the time goes:
time: 307 us; the launch traced here: 306 us
  waiting for transfers between devices  238 us (78%)
  matrix products  19 us (6%)
  local copies, waits for them, and re-layouts  18 us (6%)
  between operations  14 us (5%)
  other arithmetic  13.6 us (4%)
  starting transfers between devices  3.44 us (1%)
    all_gather x1, waiting for transfers between devices, local(): lax.all_gather(panel_blocks[0], 'zero', axis=0, tiled=True)  66.9 us
    all_gather x1, waiting for transfers between devices, local(): portion = lax.all_gather(kv_new, 'zero', axis=0, tiled=True)  64.2 us
    all_gather x1, waiting for transfers between devices, local(): cache_portion = lax.all_gather(cached_kv[0], 'zero', axis=0, tiled=True)  55 us
    ppermute x1, waiting for transfers between devices, passed_along(): return lax.ppermute(block, axis, route)  50.3 us
    dot_general x2, matrix products, absorb(): jnp.einsum('grjn,ngd->grjd', weights.astype(jnp.bfloat16), value_grid, pr...  8.01 us
    another operation x1, local copies, waits for them, and re-layouts  6.53 us
    dot_general x1, matrix products, local(): jnp.einsum('rsk,skn->rsn', chosen, lax.all_gather(panel_blocks[0], 'zero'...  6.4 us
    reduce_sum x2, other arithmetic, absorb(): new_sum = run_sum * shrink + jnp.sum(weights, axis=-1)  6.31 us
  transfers between devices with their start and end apart: 4, of which 4 were waited for; matrix products, arithmetic and copies ran while one was open for 7% of the time, Pallas kernels for 0%

commit v1 on v0

--- a/solution.py
+++ b/solution.py
@@ -70,17 +70,30 @@
         )
         return (new_max, new_sum, new_acc)
 
+    zero_size = lax.axis_size("zero")
+    local_slots = panel_blocks.shape[1]
+    weight_rows = local_slots * block_size
+    cache_local = cached_kv[0].reshape(-1, block_size)
+    packed = jnp.concatenate([panel_blocks[0].reshape(weight_rows, block_size), cache_local], axis=0)
+    gathered = lax.all_gather(packed, "zero", axis=0, tiled=True).reshape(
+        zero_size, packed.shape[0], block_size
+    )
+    all_blocks = gathered[:, :weight_rows].reshape(
+        zero_size * local_slots, block_size, block_size
+    )
+    cache_portion = gathered[:, weight_rows:].reshape(
+        zero_size * cached_kv.shape[1], cached_kv.shape[2]
+    )
     chosen = jnp.take(normed_grid, row_table, axis=1)
     slot_terms = jnp.einsum(
         "rsk,skn->rsn",
         chosen,
-        lax.all_gather(panel_blocks[0], "zero", axis=0, tiled=True),
+        all_blocks,
         preferred_element_type=jnp.float32,
     )
     slot_terms = slot_terms * slot_live[None, :, None]
     summed = slot_terms.reshape(row_count, panels, slot_depth, block_size).sum(axis=2)
     kv_new = summed.reshape(row_count, panels * block_size).astype(jnp.bfloat16)
-    cache_portion = lax.all_gather(cached_kv[0], "zero", axis=0, tiled=True)
     softmax_state = absorb(
         initial, cache_portion, jnp.ones((row_count, cache_portion.shape[0]), bool)
     )

time: 307 us -> 262 us (0.85)
  the two profiles are of different devices: /device:TPU:128 before, /device:TPU:96 now
where the time goes in v1:
time: 262 us; the launch traced here: 261 us
  waiting for transfers between devices  178 us (68%)
  matrix products  24.9 us (10%)
  local copies, waits for them, and re-layouts  21.7 us (8%)
  other arithmetic  18 us (7%)
  between operations  14.3 us (5%)
  starting transfers between devices  3.46 us (1%)
    all_gather x1, waiting for transfers between devices, local(): lax.all_gather(packed, 'zero', axis=0, tiled=True)  68.7 us
    all_gather x1, waiting for transfers between devices, local(): portion = lax.all_gather(kv_new, 'zero', axis=0, tiled=True)  58.1 us
    ppermute x1, waiting for transfers between devices, passed_along(): return lax.ppermute(block, axis, route)  51.6 us
    dot_general x2, matrix products, absorb(): jnp.einsum('grjn,ngd->grjd', weights.astype(jnp.bfloat16), value_grid, pr...  12.7 us
    dot_general x2, matrix products, absorb(): jnp.einsum('rgjd,ngd->grjn', query_grid, key_grid, preferred_element_type...  8.59 us
    reduce_sum x1, other arithmetic, absorb(): new_sum = run_sum * shrink + jnp.sum(weights, axis=-1)  8.27 us
    another operation x3, local copies, waits for them, and re-layouts  6.73 us
  transfers between devices with their start and end apart: 3, of which 3 were waited for; matrix products, arithmetic and copies ran while one was open for 5% of the time, Pallas kernels for 0%

profile of v1, /device:TPU:96, one launch (start us, length us, event | category | flops | bytes accessed | tf_op | source)
XLA Modules:
  0.0 260.9 jit_solution(13501119565918339690)
XLA Ops:
  7.2 0.0 copy-start
  7.2 0.0 copy-start.3
  7.2 0.0 copy-start.4
  7.2 0.0 all-gather.3.cloned.1.call-start
  7.2 0.8 reshape_squeeze.15
  8.1 1.6 pad_maximum_fusion
  9.7 0.0 all-gather.3.cloned.1.call-update
  9.7 0.0 all-gather.5.cloned.1.call-start
  9.8 0.8 reshape_squeeze.18
  10.5 0.8 reshape_squeeze.17
  11.3 1.1 convert_bitcast_fusion
  12.4 0.2 copy.84
  12.6 0.0 copy-done.3
  12.6 0.0 copy-done.4
  12.6 0.1 fusion.33
  12.7 0.1 reshape.143
  12.8 0.0 copy-done
  12.8 0.2 fusion.27
  13.0 0.7 fusion.30
  13.7 1.1 gather_fusion
  14.8 68.7 %all-gather.3.cloned.1.call-done = bf16[24576,128]{1,0:T(8,128)(2,1)} async-done(((bf16[768,128]{1,0:T(8,128)(2,1)}), bf16[24576,128]{1,0:T(8,128)(2,1)}) %all-gather.3.cloned.1.call-update) | async-done | bytes 6291472 | tf_op jit(solution)/shard_map/all_gather | solution.py:78
  83.5 2.8 %slice.29 = bf16[32,640,128]{2,1,0:T(8,128)(2,1)S(1)} slice(bf16[32,768,128]{2,1,0:T(8,128)(2,1)} %bitcast.70), slice={[0:32], [0:640], [0:128]} | slice | bytes 10485760 | tf_op jit(solution)/shard_map/slice | solution.py:81
  86.4 3.7 %broadcast_multiply_fusion = f32[160,128,64]{1,2,0:T(8,128)} fusion(f32[160]{0:T(256)S(1)} %reshape.143, bf16[160,128,128]{2,1,0:T(8,128)(2,1)S(1)} %bitcast.68, bf16[160,64,128]{2,1,0:T(8,128)(2,1)S(1)} %gather_fusion, pred[160]{0:T(512)(128)(4,1)S(1)} %compare_and_fusion), kind=kOutput, calls=%fused_computation.24 | convolution fusion | flops 338165760 | bytes 13108000 | tf_op jit(solution)/shard_map/rsk,skn->rsn/dot_general | solution.py:88
  90.1 0.0 copy-start.2
  90.1 3.0 %reduce_sum.38 = bf16[64,8,128]{2,0,1:T(8,128)(2,1)S(1)} reduce(f32[64,8,20,128]{3,0,2,1:T(8,128)} %bitcast.67, f32[]{:T(128)} %constant.28.clone.1), dimensions={2}, to_apply=%region_3.4 | reduce | flops 1245184 | bytes 5373956 | tf_op jit(solution)/shard_map/reduce_sum | solution.py:95
  93.1 0.7 copy_bitcast_fusion
  93.8 0.0 all-gather.5.cloned.1.call-update
  93.8 0.0 copy-done.2
  93.8 0.1 copy.83
  93.9 1.3 slice.26
  95.2 0.5 reshape.135
  95.7 0.1 fusion.37
  95.8 0.2 copy.54
  96.0 0.8 bitcast_reduce_fusion
  96.8 1.1 fusion.13
  97.9 0.1 copy.57
  98.0 1.0 copy.58
  99.0 3.4 %fusion.23 = f32[4,64,8,128]{3,2,1,0:T(8,128)} fusion(bf16[512,4,128,1]{0,2,3,1:T(8,128)(2,1)} %bitcast.78, bf16[4,64,8,512]{3,1,2,0:T(8,128)(2,1)S(1)} %get-tuple-element.81, f32[4,64,8]{2,1,0:T(8,128)S(1)} %copy.57), kind=kOutput, calls=%fused_computation.31 | convolution fusion | flops 268697600 | bytes 3678208 | tf_op jit(solution)/shard_map/grjn,ngd->grjd/dot_general | solution.py:65
  102.4 58.1 %all-gather.5.cloned.1.call-done = bf16[2048,1024]{1,0:T(8,128)(2,1)} async-done(((bf16[64,1024]{1,0:T(8,128)(2,1)}), bf16[2048,1024]{1,0:T(8,128)(2,1)}) %all-gather.5.cloned.1.call-update) | async-done | bytes 4194320 | tf_op jit(solution)/shard_map/all_gather | solution.py:100
  160.5 34.9 %conditional.1 = (f32[4,64,8]{2,1,0:T(8,128)S(1)}, f32[4,64,8,128]{3,2,1,0:T(8,128)}) conditional(s32[]{:T(128)} %convert_element_type.57, (f32[4,64,8]{1,2,0:T(8,128)S(1)}, f32[4,64,8,128]{3,2,1,0:T(8,128)}) %tuple.15, (s32[]{:T(128)}, s32[64,1]{0,1:T(1,128)S(1)}, s32[64,2048]{1,0:T(8,128)S(1)}, bf16[2048,1024]{1,0:T(8,128)(2,1)}, ...), branch_computations={%region_4.5_spmd, %region_5.8_spmd} | conditional | flops 2194280448 | bytes 75121424 | solution.py:103
  160.5 0.1 broadcast_compare_fusion
  160.7 6.6 %copy.64 = bf16[2048,1024]{0,1:T(8,128)(2,1)} copy(bf16[2048,1024]{1,0:T(8,128)(2,1)} %get-tuple-element.70) | data formatting | bytes 8388608 | tf_op jit(solution)/shard_map
  167.2 2.5 fusion.36
  169.8 7.8 %select_reduce_fusion = (f32[4,64,8]{2,1,0:T(8,128)S(1)}, f32[4,64,8,2048]{3,2,1,0:T(8,128)}) fusion(pred[64,2048]{1,0:T(8,128)(4,1)S(1)} %broadcast_compare_fusion, bf16[2048,4,128,1]{0,2,3,1:T(8,128)(2,1)S(1)} %bitcast.69, bf16[64,4,8,128]{3,2,1,0:T(8,128)(2,1)S(1)} %get-tuple-element.71), kind=kOutput, calls=%fused_computation.2 | convolution fusion | flops 1086322688 | bytes 19537920 | tf_op jit(solution)/shard_map/cond/branch_1_fun/rgjd,ngd->grjn/dot_general | solution.py:57
  177.6 0.1 copy.66
  177.7 8.3 %fusion.1 = f32[4,64,8]{2,1,0:T(8,128)S(1)} fusion(f32[4,64,8,2048]{3,2,1,0:T(8,128)} %get-tuple-element.80, f32[4,64,8]{2,1,0:T(8,128)S(1)} %max.2, pred[64,2048]{1,0:T(8,128)(4,1)S(1)} %broadcast_compare_fusion), kind=kLoop, calls=%fused_computation.4 | loop fusion | flops 16775168 | bytes 16924672 | tf_op jit(solution)/shard_map/cond/branch_1_fun/reduce_sum | solution.py:64
  186.0 0.1 copy.67
  186.1 9.3 %fusion.5 = f32[4,64,8,128]{3,2,1,0:T(8,128)} fusion(bf16[2048,4,128,1]{0,2,3,1:T(8,128)(2,1)S(1)} %bitcast.76, f32[4,64,8,2048]{3,2,1,0:T(8,128)} %get-tuple-element.80, f32[4,64,8]{2,1,0:T(8,128)S(1)} %max.2, pred[64,2048]{1,0:T(8,128)(4,1)S(1)} %broadcast_compare_fusion, f32[4,64,8,128]{3,2,1,0:T(8,128)} %get-tuple-element.32, ...), kind=kOutput, calls=%fused_computation.7 | convolution fusion | flops 1091043328 | bytes 21118976 | tf_op jit(solution)/shard_map/cond/branch_1_fun/grjn,ngd->grjd/dot_general | solution.py:65
  195.4 0.0 copy-start.1
  195.4 1.6 divide_bitcast_fusion
  197.0 0.1 copy.68
  197.1 0.2 reshape.140
  197.3 0.0 copy-done.1
  197.4 0.1 fusion.28
  197.5 3.4 %collective-permute-start = (bf16[1,64,4096]{2,1,0:T(8,128)(2,1)S(1)}, bf16[1,64,4096]{2,1,0:T(8,128)(2,1)S(1)}, u32[]{:S(2)}, u32[]{:S(2)}) collective-permute-start(bf16[1,64,4096]{2,1,0:T(8,128)(2,1)S(1)} %fusion.28), channel_id=1, source_target_pairs={{480,0},{0,32},{32,64},{64,96},{96,128},{128,160},{160,192},{192,2... | collective-permute-start | bytes 1572872 | tf_op jit(solution)/shard_map/ppermute | solution.py:16
  200.8 0.1 copy.62
  200.9 0.7 convert_element_type.67
  201.7 51.6 %collective-permute-done = bf16[1,64,4096]{2,1,0:T(8,128)(2,1)S(1)} collective-permute-done((bf16[1,64,4096]{2,1,0:T(8,128)(2,1)S(1)}, bf16[1,64,4096]{2,1,0:T(8,128)(2,1)S(1)}, u32[]{:S(2)}, u32[]{:S(2)}) %collective-permute-start) | collective-permute-done | bytes 524320 | tf_op jit(solution)/shard_map/ppermute | solution.py:16
  253.3 0.8 copy.108
  (12 shorter events, 0.2 us)
Async XLA Ops:
  7.2 5.7 %copy-start = (bf16[1,64,4096]{2,1,0:T(8,128)(2,1)S(1)}, bf16[1,64,4096]{2,1,0:T(8,128)(2,1)}, u32[]{:S(2)}) copy-start(bf16[1,64,4096]{2,1,0:T(8,128)(2,1)} %param.9) | copy-start | bytes 1572868
  7.2 5.4 %copy-start.3 = (bf16[1,4096]{1,0:T(2,128)(2,1)S(1)}, bf16[1,4096]{1,0:T(2,128)(2,1)}, u32[]{:S(2)}) copy-start(bf16[1,4096]{1,0:T(2,128)(2,1)} %param.10) | copy-start | bytes 24580
  7.2 5.5 %copy-start.4 = (s32[1,8]{1,0:T(1,128)S(1)}, s32[1,8]{1,0:T(1,128)}, u32[]{:S(2)}) copy-start(s32[1,8]{1,0:T(1,128)} %param.15) | copy-start | bytes 100
  7.2 76.3 %all-gather.3.cloned.1.call-start = ((), (), s32[]{:S(2)}) async-start(), calls=%async_computation | async-start | bytes 6488064 | tf_op jit(solution)/shard_map/all_gather | solution.py:78
  9.7 150.7 %all-gather.5.cloned.1.call-start = ((), (), s32[]{:S(2)}) async-start(), calls=%async_computation.1 | async-start | bytes 4325376 | tf_op jit(solution)/shard_map/all_gather | solution.py:100
  90.1 3.7 %copy-start.2 = (bf16[1,64,4096]{2,1,0:T(8,128)(2,1)S(1)}, bf16[1,64,4096]{2,1,0:T(8,128)(2,1)}, u32[]{:S(2)}) copy-start(bf16[1,64,4096]{2,1,0:T(8,128)(2,1)} %param.11) | copy-start | bytes 1572868
  195.4 2.0 copy-start.1
  197.5 55.8 %collective-permute-start = (bf16[1,64,4096]{2,1,0:T(8,128)(2,1)S(1)}, bf16[1,64,4096]{2,1,0:T(8,128)(2,1)S(1)}, u32[]{:S(2)}, u32[]{:S(2)}) collective-permute-start(bf16[1,64,4096]{2,1,0:T(8,128)(2,1)S(1)} %fusion.28), channel_id=1, source_target_pairs={{480,0},{0,32},{32,64},{64,96},{96,128},{128,160},{160,192},{192,2... | collective-permute-start | bytes 1572872 | tf_op jit(solution)/shard_map/ppermute | solution.py:16
Sparse Core Ops, SparseCore 0:
  10.7 72.7 all-gather.2
  93.9 66.5 all-gather.4

commit v2 on v1

v2 whole, which is shorter than its diff:
```python
import math

import jax
import jax.numpy as jnp
from jax import lax
from jax.sharding import PartitionSpec as P
from jax.experimental import pallas as pl
from jax.experimental.pallas import tpu as pltpu

QH = 32
KVH = 4
HD = 128


def passed_along(block, axis, distance):
    devices = range(lax.axis_size(axis))
    route = [((i - distance) % len(devices), i) for i in devices]
    return lax.ppermute(block, axis, route)


def attend_kernel(first_ref, q_ref, r_ref, ck_ref, cv_ref, nk_ref, nv_ref, o_ref):
    head_size = ck_ref.shape[1]
    rows = q_ref.shape[0]
    new_count = nk_ref.shape[0]
    score_scale = 1.0 / math.sqrt(head_size)
    first = first_ref[0]
    query_pos = first + lax.broadcasted_iota(jnp.int32, (rows, new_count), 0)
    key_pos = lax.broadcasted_iota(jnp.int32, (rows, new_count), 1)
    visible = key_pos <= query_pos
    cache_keys = ck_ref[...]
    new_keys = nk_ref[...]
    cache_values = cv_ref[...]
    new_values = nv_ref[...]
    contract_last = (((1,), (1,)), ((), ()))
    for head in range(q_ref.shape[1] // head_size):
        cols = pl.ds(head * head_size, head_size)
        query = q_ref[:, cols]
        cache_scores = (
            lax.dot_general(query, cache_keys, contract_last, preferred_element_type=jnp.float32)
            * score_scale
        )
        new_scores = (
            lax.dot_general(query, new_keys, contract_last, preferred_element_type=jnp.float32)
            * score_scale
        )
        new_scores = jnp.where(visible, new_scores, -jnp.inf)
        row_max = jnp.maximum(
            jnp.max(cache_scores, axis=-1, keepdims=True),
            jnp.max(new_scores, axis=-1, keepdims=True),
        )
        cache_exp = jnp.exp(cache_scores - row_max)
        new_exp = jnp.exp(new_scores - row_max)
        denominator = jnp.sum(cache_exp, axis=-1, keepdims=True) + jnp.sum(
            new_exp, axis=-1, keepdims=True
        )
        weighted = jnp.dot(
            cache_exp.astype(jnp.bfloat16), cache_values, preferred_element_type=jnp.float32
        ) + jnp.dot(new_exp.astype(jnp.bfloat16), new_values, preferred_element_type=jnp.float32)
        attended = weighted / denominator
        o_ref[:, cols] = (r_ref[:, cols].astype(jnp.float32) + attended).astype(o_ref.dtype)


def attend(first_query, queries, residual, cache_kv, new_kv):
    rows, width = queries.shape
    kv_width = cache_kv.shape[1]
    kv_heads = kv_width // (2 * HD)
    group_width = width // kv_heads
    cache_count = cache_kv.shape[0]
    new_count = new_kv.shape[0]
    keys_total = cache_count + new_count
    grid_spec = pltpu.PrefetchScalarGridSpec(
        num_scalar_prefetch=1,
        grid=(kv_heads,),
        in_specs=[
            pl.BlockSpec((rows, group_width), lambda g, f: (0, g)),
            pl.BlockSpec((rows, group_width), lambda g, f: (0, g)),
            pl.BlockSpec((cache_count, HD), lambda g, f: (0, g)),
            pl.BlockSpec((cache_count, HD), lambda g, f: (0, kv_heads + g)),
            pl.BlockSpec((new_count, HD), lambda g, f: (0, g)),
            pl.BlockSpec((new_count, HD), lambda g, f: (0, kv_heads + g)),
        ],
        out_specs=pl.BlockSpec((rows, group_width), lambda g, f: (0, g)),
    )
    return pl.pallas_call(
        attend_kernel,
        grid_spec=grid_spec,
        out_shape=jax.ShapeDtypeStruct((rows, width), jnp.bfloat16),
        cost_estimate=pl.CostEstimate(
            flops=4 * rows * (width // HD) * keys_total * HD,
            transcendentals=rows * (width // HD) * keys_total,
            bytes_accessed=2 * (3 * rows * width + keys_total * kv_width),
        ),
    )(
        first_query.reshape(1).astype(jnp.int32),
        queries,
        residual,
        cache_kv,
        cache_kv,
        new_kv,
        new_kv,
    )


def local(residual, norm_gain, queries, cached_kv, panel_blocks, block_rows, counts):
    row_count = residual.shape[1]
    model_width = residual.shape[2]
    zero_index = lax.axis_index("zero")
    zero_size = lax.axis_size("zero")
    stream = residual[0].astype(jnp.float32)
    normed = (
        stream
        * lax.rsqrt(jnp.mean(stream * stream, axis=-1, keepdims=True) + 1e-05)
        * norm_gain[0].astype(jnp.float32)
    ).astype(jnp.bfloat16)
    block_size = panel_blocks.shape[-1]
    panels = block_rows.shape[1]
    slot_depth = block_rows.shape[2]
    row_table = block_rows[0].reshape(-1)
    slot_live = (jnp.arange(slot_depth)[None, :] < counts[0][:, None]).reshape(-1)
    normed_grid = normed.reshape(row_count, model_width // block_size, block_size)
    local_slots = panel_blocks.shape[1]
    weight_rows = local_slots * block_size
    cache_local = cached_kv[0].reshape(-1, block_size)
    packed = jnp.concatenate([panel_blocks[0].reshape(weight_rows, block_size), cache_local], axis=0)
    packed_rows = packed.shape[0]
    gathered = lax.all_gather(packed, "zero", axis=0, tiled=True).reshape(
        zero_size, packed_rows, block_size
    )
    cache_portion = gathered[:, weight_rows:].reshape(
        zero_size * cached_kv.shape[1], cached_kv.shape[2]
    )
    chosen = jnp.where(slot_live[None, :, None], jnp.take(normed_grid, row_table, axis=1), 0)
    holders = zero_size // panels
    chosen = chosen.reshape(row_count, panels, holders, weight_rows)
    chosen = jnp.pad(chosen, ((0, 0), (0, 0), (0, 0), (0, packed_rows - weight_rows)))
    kv_new = jnp.einsum(
        "rphk,phkn->rpn",
        chosen,
        gathered.reshape(panels, holders, packed_rows, block_size),
        preferred_element_type=jnp.float32,
    ).reshape(row_count, panels * block_size).astype(jnp.bfloat16)
    portion = lax.all_gather(kv_new, "zero", axis=0, tiled=True)
    updated = attend(zero_index * row_count, queries[0], residual[0], cache_portion, portion)
    passed = passed_along(updated[None], "pipe", 1)
    return (passed, kv_new[None])


def solution(mesh):
    in_specs = (
        P("pipe", "zero", None),
        P("pipe", None),
        P("pipe", "zero", None),
        P("pipe", "zero", None),
        P("pipe", "zero", None, None),
        P("pipe", None, None),
        P("pipe", None),
    )
    out_specs = (P("pipe", "zero", None), P("pipe", "zero", None))
    return jax.shard_map(local, mesh=mesh, in_specs=in_specs, out_specs=out_specs, check_vma=False)
```

time: 262 us -> 240 us (0.916)
  Pallas kernels: 0 us -> 20.1 us
  matrix products: 24.9 us -> 4.83 us
  other arithmetic: 18 us -> 6.42 us
  local copies, waits for them, and re-layouts: 21.7 us -> 16.7 us
  waiting for transfers between devices: 178 us -> 174 us
    pallas_call x0 -> x1, Pallas kernels: none -> 20.1 us  [attend(): pl.pallas_call(attend_kernel, grid_spec=grid_spec, out_shape=jax.ShapeDty...]
    dot_general x5 -> x1, matrix products: 24.9 us -> 4.83 us  [local(): jnp.einsum('rphk,phkn->rpn', chosen, gathered.reshape(panels, holders, pa...]
    reduce_sum x2 -> x0, other arithmetic: 11.3 us -> none  [the longest x1 8.27 us: absorb(): new_sum = run_sum * shrink + jnp.sum(weights, axis=-1)]
    all_gather x1, waiting for transfers between devices: 68.7 us -> 57.8 us  [local(): lax.all_gather(packed, 'zero', axis=0, tiled=True)]
    gather x1 -> x3, local copies, waits for them, and re-layouts: 1.06 us -> 8.88 us  [local(): jnp.take(normed_grid, row_table, axis=1)]
    another operation x4 -> x0, local copies, waits for them, and re-layouts: 6.82 us -> none
    slice x5 -> x0, local copies, waits for them, and re-layouts: 6.67 us -> none  [the longest x3 3.62 us: absorb(): value_grid = portion[:, kv_width:].reshape(key_count, kv_heads, head_size)]
    all_gather x1, waiting for transfers between devices: 58.1 us -> 64.1 us  [local(): portion = lax.all_gather(kv_new, 'zero', axis=0, tiled=True)]
  transfers between devices with their start and end apart: 3 -> 3, of which waited for: 3 -> 3; matrix products, arithmetic and copies ran while one was open for 5% -> 8% of each run, Pallas kernels for 0% -> 0%
where the time goes in v2:
time: 240 us
  waiting for transfers between devices  174 us (72%)
  Pallas kernels  20.1 us (8%)
  local copies, waits for them, and re-layouts  16.7 us (7%)
  between operations  14.2 us (6%)
  other arithmetic  6.42 us (3%)
  matrix products  4.83 us (2%)
  starting transfers between devices  3.45 us (1%)
    all_gather x1, waiting for transfers between devices, local(): portion = lax.all_gather(kv_new, 'zero', axis=0, tiled=True)  64.1 us
    all_gather x1, waiting for transfers between devices, local(): lax.all_gather(packed, 'zero', axis=0, tiled=True)  57.8 us
    ppermute x1, waiting for transfers between devices, passed_along(): return lax.ppermute(block, axis, route)  51.8 us
    pallas_call x1, Pallas kernels, attend(): pl.pallas_call(attend_kernel, grid_spec=grid_spec, out_shape=jax.ShapeDty...  20.1 us
    gather x3, local copies, waits for them, and re-layouts, local(): jnp.take(normed_grid, row_table, axis=1)  8.88 us
    dot_general x1, matrix products, local(): jnp.einsum('rphk,phkn->rpn', chosen, gathered.reshape(panels, holders, pa...  4.83 us
  transfers between devices with their start and end apart: 3, of which 3 were waited for; matrix products, arithmetic and copies ran while one was open for 8% of the time, Pallas kernels for 0%

profile of v2, /device:TPU:96, one launch (start us, length us, event | category | flops | bytes accessed | tf_op | source)
XLA Modules:
  0.0 239.5 jit_solution(14657150869377985170)
XLA Ops:
  7.2 0.0 copy-start
  7.2 0.0 copy-start.1
  7.2 0.0 all-gather.3.cloned.1.call-start
  7.2 0.8 reshape_squeeze.12
  8.1 1.6 pad_maximum_fusion
  9.7 0.0 all-gather.3.cloned.1.call-update
  9.7 0.0 all-gather.5.cloned.1.call-start
  9.7 0.8 reshape_squeeze.14
  10.5 0.8 reshape_squeeze.13
  11.3 1.1 convert_bitcast_fusion
  12.4 0.2 copy.27
  12.6 0.0 copy-done.1
  12.6 0.0 copy-done
  12.7 0.2 multiply_reduce_fusion
  12.9 0.7 fusion.10
  13.6 1.1 gather_fusion
  14.6 3.3 %copy.21 = bf16[64,160,128]{2,1,0:T(8,128)(2,1)} copy(bf16[64,160,128]{2,0,1:T(8,128)(2,1)S(1)} %bitcast.32) | data formatting | bytes 5242880 | tf_op jit(solution)/shard_map/jit(_take)/gather | solution.py:132
  17.9 0.0 copy-start.2
  17.9 4.6 %gather.7 = bf16[64,8,4,640]{3,2,1,0:T(4,128)(2,1)S(1)} reshape(bf16[64,160,128]{2,1,0:T(8,128)(2,1)} %copy.21) | data formatting | bytes 5242880 | tf_op jit(solution)/shard_map/jit(_take)/gather | solution.py:132
  22.5 0.1 broadcast_in_dim.40
  22.6 0.1 broadcast_in_dim.41
  22.7 0.0 copy-done.2
  22.7 0.1 add_compare_fusion
  22.8 0.1 broadcast_in_dim.37
  22.9 0.1 broadcast_in_dim.38
  23.0 2.7 %fusion.2 = bf16[64,8,4,640]{3,0,2,1:T(8,128)(2,1)} fusion(bf16[64,8,4,640]{3,2,1,0:T(4,128)(2,1)S(1)} %gather.7, pred[8,4,640]{2,1,0:T(4,128)(4,1)S(1)} %copy.19, pred[8,4,640]{2,1,0:T(4,128)(4,1)S(1)} %copy.17), kind=kLoop, calls=%fused_computation.4 | loop fusion | flops 2621440 | bytes 5283840 | tf_op jit(solution)/shard_map/jit(_where)/select_n | solution.py:132
  25.7 57.8 %all-gather.3.cloned.1.call-done = bf16[24576,128]{1,0:T(8,128)(2,1)} async-done(((bf16[768,128]{1,0:T(8,128)(2,1)}), bf16[24576,128]{1,0:T(8,128)(2,1)}) %all-gather.3.cloned.1.call-update) | async-done | bytes 6291472 | tf_op jit(solution)/shard_map/all_gather | solution.py:126
  83.5 4.8 %fusion.6 = bf16[8,128,64]{1,2,0:T(8,128)(2,1)S(1)} fusion(bf16[8,4,768,128]{3,2,1,0:T(8,128)(2,1)} %bitcast.33, bf16[64,8,4,640]{3,0,2,1:T(8,128)(2,1)} %fusion.2), kind=kOutput, calls=%fused_computation.6 | convolution fusion | flops 402718720 | bytes 9043968 | tf_op jit(solution)/shard_map/rphk,phkn->rpn/dot_general | solution.py:136
  88.4 0.7 copy_bitcast_fusion
  89.0 0.0 all-gather.5.cloned.1.call-update
  89.1 1.3 slice.6
  90.4 1.3 reshape.114.ck_ref.cv_ref
  91.7 64.1 %all-gather.5.cloned.1.call-done.nk_ref.nv_ref = bf16[2048,1024]{1,0:T(8,128)(2,1)} async-done(((bf16[64,1024]{1,0:T(8,128)(2,1)}), bf16[2048,1024]{1,0:T(8,128)(2,1)}) %all-gather.5.cloned.1.call-update) | async-done | bytes 4194320 | tf_op jit(solution)/shard_map/all_gather | solution.py:142
  155.7 20.1 %shard_map.86 = bf16[64,4096]{1,0:T(8,128)(2,1)} custom-call(s32[1]{0:T(128)} %bitcast.first_ref, bf16[64,4096]{1,0:T(8,128)(2,1)} %bitcast.38, bf16[64,4096]{1,0:T(8,128)(2,1)} %bitcast.35, bf16[512,1024]{1,0:T(8,128)(2,1)} %reshape.114.ck_ref.cv_ref, bf16[512,1024]{1,0:T(8,128)(2,1)} %reshape.114.ck_ref.cv_ref, ...), custom_call_target="tpu_custom_call" | custom-call | flops 2684354560 | bytes 6815744 | tf_op jit(solution)/shard_map/pallas_call | solution.py:84
  175.8 3.4 %collective-permute-start = (bf16[1,64,4096]{2,1,0:T(8,128)(2,1)}, bf16[1,64,4096]{2,1,0:T(8,128)(2,1)S(1)}, u32[]{:S(2)}, u32[]{:S(2)}) collective-permute-start(bf16[1,64,4096]{2,1,0:T(8,128)(2,1)} %bitcast.39), channel_id=1, source_target_pairs={{480,0},{0,32},{32,64},{64,96},{96,128},{128,160},{160,192},{192,2... | collective-permute-start | bytes 1572872 | tf_op jit(solution)/shard_map/ppermute | solution.py:18
  179.2 0.1 copy.23
  179.3 0.7 convert_element_type.46
  180.0 51.8 %collective-permute-done = bf16[1,64,4096]{2,1,0:T(8,128)(2,1)S(1)} collective-permute-done((bf16[1,64,4096]{2,1,0:T(8,128)(2,1)}, bf16[1,64,4096]{2,1,0:T(8,128)(2,1)S(1)}, u32[]{:S(2)}, u32[]{:S(2)}) %collective-permute-start) | collective-permute-done | bytes 524320 | tf_op jit(solution)/shard_map/ppermute | solution.py:18
  231.9 0.8 copy.38
  (8 shorter events, 0.1 us)
Async XLA Ops:
  7.2 5.5 %copy-start = (bf16[1,64,4096]{2,1,0:T(8,128)(2,1)S(1)}, bf16[1,64,4096]{2,1,0:T(8,128)(2,1)}, u32[]{:S(2)}) copy-start(bf16[1,64,4096]{2,1,0:T(8,128)(2,1)} %param.7) | copy-start | bytes 1572868
  7.2 5.4 %copy-start.1 = (bf16[1,4096]{1,0:T(2,128)(2,1)S(1)}, bf16[1,4096]{1,0:T(2,128)(2,1)}, u32[]{:S(2)}) copy-start(bf16[1,4096]{1,0:T(2,128)(2,1)} %param.8) | copy-start | bytes 24580
  7.2 76.3 %all-gather.3.cloned.1.call-start = ((), (), s32[]{:S(2)}) async-start(), calls=%async_computation | async-start | bytes 6488064 | tf_op jit(solution)/shard_map/all_gather | solution.py:126
  9.7 146.0 %all-gather.5.cloned.1.call-start = ((), (), s32[]{:S(2)}) async-start(), calls=%async_computation.1 | async-start | bytes 4325376 | tf_op jit(solution)/shard_map/all_gather | solution.py:142
  17.9 4.8 %copy-start.2 = (s32[1,8]{1,0:T(1,128)S(1)}, s32[1,8]{1,0:T(1,128)}, u32[]{:S(2)}) copy-start(s32[1,8]{1,0:T(1,128)} %param.13) | copy-start | bytes 100
  175.8 56.0 %collective-permute-start = (bf16[1,64,4096]{2,1,0:T(8,128)(2,1)}, bf16[1,64,4096]{2,1,0:T(8,128)(2,1)S(1)}, u32[]{:S(2)}, u32[]{:S(2)}) collective-permute-start(bf16[1,64,4096]{2,1,0:T(8,128)(2,1)} %bitcast.39), channel_id=1, source_target_pairs={{480,0},{0,32},{32,64},{64,96},{96,128},{128,160},{160,192},{192,2... | collective-permute-start | bytes 1572872 | tf_op jit(solution)/shard_map/ppermute | solution.py:18
Sparse Core Ops, SparseCore 0:
  10.7 72.7 all-gather.2
  89.2 66.5 all-gather.4

commit v3 on v2

--- a/solution.py
+++ b/solution.py
@@ -60,7 +60,7 @@
         o_ref[:, cols] = (r_ref[:, cols].astype(jnp.float32) + attended).astype(o_ref.dtype)
 
 
-def attend(first_query, queries, residual, cache_kv, new_kv):
+def attend_group(group, first_query, queries, residual, cache_kv, new_kv):
     rows, width = queries.shape
     kv_width = cache_kv.shape[1]
     kv_heads = kv_width // (2 * HD)
@@ -70,25 +70,26 @@
     keys_total = cache_count + new_count
     grid_spec = pltpu.PrefetchScalarGridSpec(
         num_scalar_prefetch=1,
-        grid=(kv_heads,),
+        grid=(1,),
         in_specs=[
-            pl.BlockSpec((rows, group_width), lambda g, f: (0, g)),
-            pl.BlockSpec((rows, group_width), lambda g, f: (0, g)),
-            pl.BlockSpec((cache_count, HD), lambda g, f: (0, g)),
-            pl.BlockSpec((cache_count, HD), lambda g, f: (0, kv_heads + g)),
-            pl.BlockSpec((new_count, HD), lambda g, f: (0, g)),
-            pl.BlockSpec((new_count, HD), lambda g, f: (0, kv_heads + g)),
+            pl.BlockSpec((rows, group_width), lambda i, f: (0, group)),
+            pl.BlockSpec((rows, group_width), lambda i, f: (0, group)),
+            pl.BlockSpec((cache_count, HD), lambda i, f: (0, group)),
+            pl.BlockSpec((cache_count, HD), lambda i, f: (0, kv_heads + group)),
+            pl.BlockSpec((new_count, HD), lambda i, f: (0, group)),
+            pl.BlockSpec((new_count, HD), lambda i, f: (0, kv_heads + group)),
         ],
-        out_specs=pl.BlockSpec((rows, group_width), lambda g, f: (0, g)),
+        out_specs=pl.BlockSpec((rows, group_width), lambda i, f: (0, 0)),
     )
+    heads = group_width // HD
     return pl.pallas_call(
         attend_kernel,
         grid_spec=grid_spec,
-        out_shape=jax.ShapeDtypeStruct((rows, width), jnp.bfloat16),
+        out_shape=jax.ShapeDtypeStruct((rows, group_width), jnp.bfloat16),
         cost_estimate=pl.CostEstimate(
-            flops=4 * rows * (width // HD) * keys_total * HD,
-            transcendentals=rows * (width // HD) * keys_total,
-            bytes_accessed=2 * (3 * rows * width + keys_total * kv_width),
+            flops=4 * rows * heads * keys_total * HD,
+            transcendentals=rows * heads * keys_total,
+            bytes_accessed=2 * (3 * rows * group_width + 2 * keys_total * HD),
         ),
     )(
         first_query.reshape(1).astype(jnp.int32),
@@ -140,8 +141,19 @@
         preferred_element_type=jnp.float32,
     ).reshape(row_count, panels * block_size).astype(jnp.bfloat16)
     portion = lax.all_gather(kv_new, "zero", axis=0, tiled=True)
-    updated = attend(zero_index * row_count, queries[0], residual[0], cache_portion, portion)
-    passed = passed_along(updated[None], "pipe", 1)
+    passed = jnp.concatenate(
+        [
+            passed_along(
+                attend_group(
+                    group, zero_index * row_count, queries[0], residual[0], cache_portion, portion
+                )[None],
+                "pipe",
+                1,
+            )
+            for group in range(cached_kv.shape[2] // (2 * HD))
+        ],
+        axis=-1,
+    )
     return (passed, kv_new[None])
 
 

time: 240 us -> 229 us (0.954)
  the two profiles are of different devices: /device:TPU:96 before, /device:TPU:99 now
where the time goes in v3:
time: 229 us; the launch traced here: 228 us
  waiting for transfers between devices  143 us (62%)
  Pallas kernels  26.4 us (12%)
  starting transfers between devices  16.6 us (7%)
  local copies, waits for them, and re-layouts  15.9 us (7%)
  between operations  14.3 us (6%)
  other arithmetic  7.25 us (3%)
  matrix products  4.82 us (2%)
    all_gather x1, waiting for transfers between devices, local(): portion = lax.all_gather(kv_new, 'zero', axis=0, tiled=True)  64.4 us
    all_gather x1, waiting for transfers between devices, local(): lax.all_gather(packed, 'zero', axis=0, tiled=True)  57.2 us
    pallas_call x4, Pallas kernels, attend_group(): pl.pallas_call(attend_kernel, grid_spec=grid_spec, out_shape=jax.ShapeDty...  26.4 us
    ppermute x4, waiting for transfers between devices, passed_along(): return lax.ppermute(block, axis, route)  21.6 us
    ppermute x4, starting transfers between devices, passed_along(): return lax.ppermute(block, axis, route)  16.6 us
    gather x3, local copies, waits for them, and re-layouts, local(): jnp.take(normed_grid, row_table, axis=1)  8.88 us
    dot_general x1, matrix products, local(): jnp.einsum('rphk,phkn->rpn', chosen, gathered.reshape(panels, holders, pa...  4.82 us
  transfers between devices with their start and end apart: 6, of which 3 were waited for; matrix products, arithmetic and copies ran while one was open for 8% of the time, Pallas kernels for 9%

profile of v3, /device:TPU:99, one launch (start us, length us, event | category | flops | bytes accessed | tf_op | source)
XLA Modules:
  0.0 228.5 jit_solution(10946574946968517254)
XLA Ops:
  7.2 0.0 copy-start
  7.2 0.0 copy-start.1
  7.2 0.0 all-gather.3.cloned.1.call-start
  7.2 0.8 reshape_squeeze.12
  8.1 1.6 pad_maximum_fusion.1
  9.7 0.0 all-gather.3.cloned.1.call-update
  9.7 0.0 all-gather.5.cloned.1.call-start
  9.7 0.8 reshape_squeeze.14
  10.5 0.8 reshape_squeeze.13
  11.3 1.1 convert_bitcast_fusion
  12.4 0.2 copy.27
  12.6 0.0 copy-done.1
  12.6 0.0 copy-done
  12.7 0.2 multiply_reduce_fusion
  12.9 0.7 fusion.10
  13.6 1.1 gather_fusion
  14.6 3.3 %copy.21 = bf16[64,160,128]{2,1,0:T(8,128)(2,1)} copy(bf16[64,160,128]{2,0,1:T(8,128)(2,1)S(1)} %bitcast.39) | data formatting | bytes 5242880 | tf_op jit(solution)/shard_map/jit(_take)/gather | solution.py:133
  17.9 0.0 copy-start.2
  17.9 4.6 %gather.7 = bf16[64,8,4,640]{3,2,1,0:T(4,128)(2,1)S(1)} reshape(bf16[64,160,128]{2,1,0:T(8,128)(2,1)} %copy.21) | data formatting | bytes 5242880 | tf_op jit(solution)/shard_map/jit(_take)/gather | solution.py:133
  22.5 0.1 broadcast_in_dim.49
  22.6 0.1 broadcast_in_dim.50
  22.7 0.0 copy-done.2
  22.7 0.1 add_compare_fusion
  22.8 0.1 broadcast_in_dim.46
  22.9 0.1 broadcast_in_dim.47
  23.0 2.7 %fusion.2 = bf16[64,8,4,640]{3,0,2,1:T(8,128)(2,1)} fusion(bf16[64,8,4,640]{3,2,1,0:T(4,128)(2,1)S(1)} %gather.7, pred[8,4,640]{2,1,0:T(4,128)(4,1)S(1)} %copy.19, pred[8,4,640]{2,1,0:T(4,128)(4,1)S(1)} %copy.17), kind=kLoop, calls=%fused_computation.4 | loop fusion | flops 2621440 | bytes 5283840 | tf_op jit(solution)/shard_map/jit(_where)/select_n | solution.py:133
  25.7 57.2 %all-gather.3.cloned.1.call-done = bf16[24576,128]{1,0:T(8,128)(2,1)} async-done(((bf16[768,128]{1,0:T(8,128)(2,1)}), bf16[24576,128]{1,0:T(8,128)(2,1)}) %all-gather.3.cloned.1.call-update) | async-done | bytes 6291472 | tf_op jit(solution)/shard_map/all_gather | solution.py:127
  82.8 4.8 %fusion.6 = bf16[8,128,64]{1,2,0:T(8,128)(2,1)S(1)} fusion(bf16[8,4,768,128]{3,2,1,0:T(8,128)(2,1)} %bitcast.40, bf16[64,8,4,640]{3,0,2,1:T(8,128)(2,1)} %fusion.2), kind=kOutput, calls=%fused_computation.6 | convolution fusion | flops 402718720 | bytes 9043968 | tf_op jit(solution)/shard_map/rphk,phkn->rpn/dot_general | solution.py:137
  87.7 0.7 copy_bitcast_fusion
  88.4 0.0 all-gather.5.cloned.1.call-update
  88.4 1.3 slice.6
  89.7 1.3 reshape.117.ck_ref.cv_ref
  91.0 64.4 %all-gather.5.cloned.1.call-done.nk_ref.nv_ref = bf16[2048,1024]{1,0:T(8,128)(2,1)} async-done(((bf16[64,1024]{1,0:T(8,128)(2,1)}), bf16[2048,1024]{1,0:T(8,128)(2,1)}) %all-gather.5.cloned.1.call-update) | async-done | bytes 4194320 | tf_op jit(solution)/shard_map/all_gather | solution.py:143
  155.4 6.6 %shard_map.86 = bf16[64,1024]{1,0:T(8,128)(2,1)} custom-call(s32[1]{0:T(128)} %bitcast.first_ref, bf16[64,4096]{1,0:T(8,128)(2,1)} %bitcast.42, bf16[64,4096]{1,0:T(8,128)(2,1)} %bitcast.35, bf16[512,1024]{1,0:T(8,128)(2,1)} %reshape.117.ck_ref.cv_ref, bf16[512,1024]{1,0:T(8,128)(2,1)} %reshape.117.ck_ref.cv_ref, ...), custom_call_target="tpu_custom_call" | custom-call | flops 671088640 | bytes 1703936 | tf_op jit(solution)/shard_map/pallas_call | solution.py:85
  162.0 3.3 %collective-permute-start = (bf16[1,64,1024]{2,1,0:T(8,128)(2,1)}, bf16[1,64,1024]{2,1,0:T(8,128)(2,1)S(1)}, u32[]{:S(2)}, u32[]{:S(2)}) collective-permute-start(bf16[1,64,1024]{2,1,0:T(8,128)(2,1)} %bitcast.49), channel_id=1, source_target_pairs={{480,0},{0,32},{32,64},{64,96},{96,128},{128,160},{160,192},{192,2... | collective-permute-start | bytes 393224 | tf_op jit(solution)/shard_map/ppermute | solution.py:18
  165.2 6.6 %shard_map.87 = bf16[64,1024]{1,0:T(8,128)(2,1)} custom-call(s32[1]{0:T(128)} %bitcast.first_ref, bf16[64,4096]{1,0:T(8,128)(2,1)} %bitcast.43, bf16[64,4096]{1,0:T(8,128)(2,1)} %bitcast.36, bf16[512,1024]{1,0:T(8,128)(2,1)} %reshape.117.ck_ref.cv_ref, bf16[512,1024]{1,0:T(8,128)(2,1)} %reshape.117.ck_ref.cv_ref, ...), custom_call_target="tpu_custom_call" | custom-call | flops 671088640 | bytes 1703936 | tf_op jit(solution)/shard_map/pallas_call | solution.py:85
  171.9 3.2 %collective-permute-start.1 = (bf16[1,64,1024]{2,1,0:T(8,128)(2,1)}, bf16[1,64,1024]{2,1,0:T(8,128)(2,1)S(1)}, u32[]{:S(2)}, u32[]{:S(2)}) collective-permute-start(bf16[1,64,1024]{2,1,0:T(8,128)(2,1)} %bitcast.50), channel_id=1, source_target_pairs={{480,0},{0,32},{32,64},{64,96},{96,128},{128,160},{160,192},{192,2... | collective-permute-start | bytes 393224 | tf_op jit(solution)/shard_map/ppermute | solution.py:18
  175.1 6.6 %shard_map.88 = bf16[64,1024]{1,0:T(8,128)(2,1)} custom-call(s32[1]{0:T(128)} %bitcast.first_ref, bf16[64,4096]{1,0:T(8,128)(2,1)} %bitcast.44, bf16[64,4096]{1,0:T(8,128)(2,1)} %bitcast.37, bf16[512,1024]{1,0:T(8,128)(2,1)} %reshape.117.ck_ref.cv_ref, bf16[512,1024]{1,0:T(8,128)(2,1)} %reshape.117.ck_ref.cv_ref, ...), custom_call_target="tpu_custom_call" | custom-call | flops 671088640 | bytes 1703936 | tf_op jit(solution)/shard_map/pallas_call | solution.py:85
  181.7 2.7 %collective-permute-start.2 = (bf16[1,64,1024]{2,1,0:T(8,128)(2,1)}, bf16[1,64,1024]{2,1,0:T(8,128)(2,1)S(1)}, u32[]{:S(2)}, u32[]{:S(2)}) collective-permute-start(bf16[1,64,1024]{2,1,0:T(8,128)(2,1)} %bitcast.51), channel_id=1, source_target_pairs={{480,0},{0,32},{32,64},{64,96},{96,128},{128,160},{160,192},{192,2... | collective-permute-start | bytes 393224 | tf_op jit(solution)/shard_map/ppermute | solution.py:18
  184.4 6.6 %shard_map.89 = bf16[64,1024]{1,0:T(8,128)(2,1)} custom-call(s32[1]{0:T(128)} %bitcast.first_ref, bf16[64,4096]{1,0:T(8,128)(2,1)} %bitcast.45, bf16[64,4096]{1,0:T(8,128)(2,1)} %bitcast.38, bf16[512,1024]{1,0:T(8,128)(2,1)} %reshape.117.ck_ref.cv_ref, bf16[512,1024]{1,0:T(8,128)(2,1)} %reshape.117.ck_ref.cv_ref, ...), custom_call_target="tpu_custom_call" | custom-call | flops 671088640 | bytes 1703936 | tf_op jit(solution)/shard_map/pallas_call | solution.py:85
  191.0 7.4 %collective-permute-start.3 = (bf16[1,64,1024]{2,1,0:T(8,128)(2,1)}, bf16[1,64,1024]{2,1,0:T(8,128)(2,1)S(1)}, u32[]{:S(2)}, u32[]{:S(2)}) collective-permute-start(bf16[1,64,1024]{2,1,0:T(8,128)(2,1)} %bitcast.52), channel_id=1, source_target_pairs={{480,0},{0,32},{32,64},{64,96},{96,128},{128,160},{160,192},{192,2... | collective-permute-start | bytes 393224 | tf_op jit(solution)/shard_map/ppermute | solution.py:18
  198.3 0.1 copy.23
  198.4 0.7 convert_element_type.46
  199.2 0.0 collective-permute-done
  199.2 0.0 collective-permute-done.1
  199.2 0.0 collective-permute-done.2
  199.2 21.6 %collective-permute-done.3 = bf16[1,64,1024]{2,1,0:T(8,128)(2,1)S(1)} collective-permute-done((bf16[1,64,1024]{2,1,0:T(8,128)(2,1)}, bf16[1,64,1024]{2,1,0:T(8,128)(2,1)S(1)}, u32[]{:S(2)}, u32[]{:S(2)}) %collective-permute-start.3) | collective-permute-done | bytes 131104 | tf_op jit(solution)/shard_map/ppermute | solution.py:18
  220.8 0.8 pad_maximum_fusion
  (8 shorter events, 0.1 us)
Async XLA Ops:
  7.2 5.5 %copy-start = (bf16[1,64,4096]{2,1,0:T(8,128)(2,1)S(1)}, bf16[1,64,4096]{2,1,0:T(8,128)(2,1)}, u32[]{:S(2)}) copy-start(bf16[1,64,4096]{2,1,0:T(8,128)(2,1)} %param.7) | copy-start | bytes 1572868
  7.2 5.4 %copy-start.1 = (bf16[1,4096]{1,0:T(2,128)(2,1)S(1)}, bf16[1,4096]{1,0:T(2,128)(2,1)}, u32[]{:S(2)}) copy-start(bf16[1,4096]{1,0:T(2,128)(2,1)} %param.8) | copy-start | bytes 24580
  7.2 75.7 %all-gather.3.cloned.1.call-start = ((), (), s32[]{:S(2)}) async-start(), calls=%async_computation | async-start | bytes 6488064 | tf_op jit(solution)/shard_map/all_gather | solution.py:127
  9.7 145.7 %all-gather.5.cloned.1.call-start = ((), (), s32[]{:S(2)}) async-start(), calls=%async_computation.1 | async-start | bytes 4325376 | tf_op jit(solution)/shard_map/all_gather | solution.py:143
  17.9 4.8 %copy-start.2 = (s32[1,8]{1,0:T(1,128)S(1)}, s32[1,8]{1,0:T(1,128)}, u32[]{:S(2)}) copy-start(s32[1,8]{1,0:T(1,128)} %param.13) | copy-start | bytes 100
  162.0 37.2 %collective-permute-start = (bf16[1,64,1024]{2,1,0:T(8,128)(2,1)}, bf16[1,64,1024]{2,1,0:T(8,128)(2,1)S(1)}, u32[]{:S(2)}, u32[]{:S(2)}) collective-permute-start(bf16[1,64,1024]{2,1,0:T(8,128)(2,1)} %bitcast.49), channel_id=1, source_target_pairs={{480,0},{0,32},{32,64},{64,96},{96,128},{128,160},{160,192},{192,2... | collective-permute-start | bytes 393224 | tf_op jit(solution)/shard_map/ppermute | solution.py:18
  171.9 27.3 %collective-permute-start.1 = (bf16[1,64,1024]{2,1,0:T(8,128)(2,1)}, bf16[1,64,1024]{2,1,0:T(8,128)(2,1)S(1)}, u32[]{:S(2)}, u32[]{:S(2)}) collective-permute-start(bf16[1,64,1024]{2,1,0:T(8,128)(2,1)} %bitcast.50), channel_id=1, source_target_pairs={{480,0},{0,32},{32,64},{64,96},{96,128},{128,160},{160,192},{192,2... | collective-permute-start | bytes 393224 | tf_op jit(solution)/shard_map/ppermute | solution.py:18
  181.7 17.5 %collective-permute-start.2 = (bf16[1,64,1024]{2,1,0:T(8,128)(2,1)}, bf16[1,64,1024]{2,1,0:T(8,128)(2,1)S(1)}, u32[]{:S(2)}, u32[]{:S(2)}) collective-permute-start(bf16[1,64,1024]{2,1,0:T(8,128)(2,1)} %bitcast.51), channel_id=1, source_target_pairs={{480,0},{0,32},{32,64},{64,96},{96,128},{128,160},{160,192},{192,2... | collective-permute-start | bytes 393224 | tf_op jit(solution)/shard_map/ppermute | solution.py:18
  191.0 29.8 %collective-permute-start.3 = (bf16[1,64,1024]{2,1,0:T(8,128)(2,1)}, bf16[1,64,1024]{2,1,0:T(8,128)(2,1)S(1)}, u32[]{:S(2)}, u32[]{:S(2)}) collective-permute-start(bf16[1,64,1024]{2,1,0:T(8,128)(2,1)} %bitcast.52), channel_id=1, source_target_pairs={{480,0},{0,32},{32,64},{64,96},{96,128},{128,160},{160,192},{192,2... | collective-permute-start | bytes 393224 | tf_op jit(solution)/shard_map/ppermute | solution.py:18
Sparse Core Ops, SparseCore 0:
  10.7 72.0 all-gather.2
  88.5 66.8 all-gather.4

commit v4 on v3

v4 whole, which is shorter than its diff:
```python
import functools
import math

import jax
import jax.numpy as jnp
from jax import lax
from jax.sharding import PartitionSpec as P
from jax.experimental import pallas as pl
from jax.experimental.pallas import tpu as pltpu

QH = 32
KVH = 4
HD = 128


def passed_along(block, axis, distance):
    devices = range(lax.axis_size(axis))
    route = [((i - distance) % len(devices), i) for i in devices]
    return lax.ppermute(block, axis, route)


def attend_kernel(first_ref, pos_ref, q_ref, r_ref, k_ref, v_ref, o_ref, *, stack):
    rows = q_ref.shape[0]
    score_scale = 1.0 / math.sqrt(HD)
    keys = k_ref[...]
    values = v_ref[...]
    key_pos = pos_ref[...]
    stacked = stack * rows
    query_pos = first_ref[0] + jnp.bitwise_and(
        lax.broadcasted_iota(jnp.int32, (stacked, 1), 0), rows - 1
    )
    visible = key_pos <= query_pos
    contract_last = (((1,), (1,)), ((), ()))
    for first_head in range(0, q_ref.shape[1] // HD, stack):
        heads = range(first_head, first_head + stack)
        query = jnp.concatenate([q_ref[:, pl.ds(h * HD, HD)] for h in heads], axis=0)
        scores = (
            lax.dot_general(query, keys, contract_last, preferred_element_type=jnp.float32)
            * score_scale
        )
        scores = jnp.where(visible, scores, -jnp.inf)
        row_max = jnp.max(scores, axis=-1, keepdims=True)
        exp_scores = jnp.exp(scores - row_max)
        denominator = jnp.sum(exp_scores, axis=-1, keepdims=True)
        attended = (
            jnp.dot(exp_scores.astype(jnp.bfloat16), values, preferred_element_type=jnp.float32)
            / denominator
        )
        for i, h in enumerate(heads):
            cols = pl.ds(h * HD, HD)
            o_ref[:, cols] = (
                r_ref[:, cols].astype(jnp.float32) + attended[i * rows : (i + 1) * rows]
            ).astype(o_ref.dtype)


def attend_group(group, first_query, key_pos, queries, residual, every_kv):
    rows, width = queries.shape
    key_count, kv_width = every_kv.shape
    kv_heads = kv_width // (2 * HD)
    group_width = width // kv_heads
    heads = group_width // HD
    grid_spec = pltpu.PrefetchScalarGridSpec(
        num_scalar_prefetch=1,
        grid=(1,),
        in_specs=[
            pl.BlockSpec((1, key_count), lambda i, f: (0, 0)),
            pl.BlockSpec((rows, group_width), lambda i, f: (0, group)),
            pl.BlockSpec((rows, group_width), lambda i, f: (0, group)),
            pl.BlockSpec((key_count, HD), lambda i, f: (0, group)),
            pl.BlockSpec((key_count, HD), lambda i, f: (0, kv_heads + group)),
        ],
        out_specs=pl.BlockSpec((rows, group_width), lambda i, f: (0, 0)),
    )
    return pl.pallas_call(
        functools.partial(attend_kernel, stack=4),
        grid_spec=grid_spec,
        out_shape=jax.ShapeDtypeStruct((rows, group_width), jnp.bfloat16),
        compiler_params=pltpu.CompilerParams(vmem_limit_bytes=48 * 1024 * 1024),
        cost_estimate=pl.CostEstimate(
            flops=4 * rows * heads * key_count * HD,
            transcendentals=rows * heads * key_count,
            bytes_accessed=2 * (3 * rows * group_width + 2 * key_count * HD),
        ),
    )(first_query.reshape(1).astype(jnp.int32), key_pos, queries, residual, every_kv, every_kv)


def local(residual, norm_gain, queries, cached_kv, panel_blocks, block_rows, counts):
    row_count = residual.shape[1]
    model_width = residual.shape[2]
    zero_index = lax.axis_index("zero")
    zero_size = lax.axis_size("zero")
    stream = residual[0].astype(jnp.float32)
    normed = (
        stream
        * lax.rsqrt(jnp.mean(stream * stream, axis=-1, keepdims=True) + 1e-05)
        * norm_gain[0].astype(jnp.float32)
    ).astype(jnp.bfloat16)
    block_size = panel_blocks.shape[-1]
    panels = block_rows.shape[1]
    slot_depth = block_rows.shape[2]
    row_table = block_rows[0].reshape(-1)
    slot_live = (jnp.arange(slot_depth)[None, :] < counts[0][:, None]).reshape(-1)
    normed_grid = normed.reshape(row_count, model_width // block_size, block_size)
    every_block = lax.all_gather(panel_blocks[0], "zero", axis=0, tiled=True)
    chosen = jnp.where(slot_live[None, :, None], jnp.take(normed_grid, row_table, axis=1), 0)
    kv_new = jnp.einsum(
        "rpk,pkn->rpn",
        chosen.reshape(row_count, panels, slot_depth * block_size),
        every_block.reshape(panels, slot_depth * block_size, block_size),
        preferred_element_type=jnp.float32,
    ).reshape(row_count, panels * block_size).astype(jnp.bfloat16)
    cache_rows = cached_kv.shape[1]
    every_kv = lax.all_gather(
        jnp.concatenate([kv_new, cached_kv[0]], axis=0), "zero", axis=0, tiled=True
    )
    piece = jnp.arange(row_count + cache_rows)
    key_pos = jnp.where(
        piece[None, :] < row_count,
        jnp.arange(zero_size)[:, None] * row_count + piece[None, :],
        -1,
    ).reshape(1, -1)
    first_query = zero_index * row_count
    passed = jnp.concatenate(
        [
            passed_along(
                attend_group(group, first_query, key_pos, queries[0], residual[0], every_kv)[None],
                "pipe",
                1,
            )
            for group in range(cached_kv.shape[2] // (2 * HD))
        ],
        axis=-1,
    )
    return (passed, kv_new[None])


def solution(mesh):
    in_specs = (
        P("pipe", "zero", None),
        P("pipe", None),
        P("pipe", "zero", None),
        P("pipe", "zero", None),
        P("pipe", "zero", None, None),
        P("pipe", None, None),
        P("pipe", None),
    )
    out_specs = (P("pipe", "zero", None), P("pipe", "zero", None))
    return jax.shard_map(local, mesh=mesh, in_specs=in_specs, out_specs=out_specs, check_vma=False)
```

time: 229 us -> 228 us (level)
  the two profiles are of different devices: /device:TPU:99 before, /device:TPU:3 now
where the time goes in v4:
time: 228 us
  waiting for transfers between devices  156 us (68%)
  starting transfers between devices  16.6 us (7%)
  Pallas kernels  15.2 us (7%)
  local copies, waits for them, and re-layouts  14.5 us (6%)
  between operations  14.3 us (6%)
  other arithmetic  6.11 us (3%)
  matrix products  5.15 us (2%)
    all_gather x1, waiting for transfers between devices, local(): lax.all_gather(jnp.concatenate([kv_new, cached_kv[0]], axis=0), 'zero', a...  68.1 us
    all_gather x1, waiting for transfers between devices, local(): every_block = lax.all_gather(panel_blocks[0], 'zero', axis=0, tiled=True)  57.7 us
    ppermute x4, waiting for transfers between devices, passed_along(): return lax.ppermute(block, axis, route)  29.4 us
    ppermute x4, starting transfers between devices, passed_along(): return lax.ppermute(block, axis, route)  16.5 us
    pallas_call x4, Pallas kernels, attend_group(): pl.pallas_call(functools.partial(attend_kernel, stack=4), grid_spec=grid_...  15.2 us
    gather x3, local copies, waits for them, and re-layouts, local(): jnp.take(normed_grid, row_table, axis=1)  12.4 us
    dot_general x1, matrix products, local(): jnp.einsum('rpk,pkn->rpn', chosen.reshape(row_count, panels, slot_depth *...  5.15 us
  transfers between devices with their start and end apart: 6, of which 5 were waited for; matrix products, arithmetic and copies ran while one was open for 8% of the time, Pallas kernels for 5%

profile of v4, /device:TPU:3, one launch (start us, length us, event | category | flops | bytes accessed | tf_op | source)
XLA Modules:
  0.0 227.7 jit_solution(4052833857647066060)
XLA Ops:
  7.2 0.0 copy-start
  7.2 0.0 copy-start.3
  7.2 0.0 all-gather.6.cloned.1.call-start
  7.2 0.7 all-gather.6.cloned.1.call-update
  7.9 0.0 all-gather.4.cloned.1.call-start
  8.0 0.8 reshape_squeeze.6
  8.7 0.7 compare_and_fusion
  9.4 0.1 copy.22
  9.5 1.1 convert_bitcast_fusion
  10.6 0.2 copy.30
  10.8 0.0 copy-done.3
  10.9 0.0 copy-done
  10.9 0.2 multiply_reduce_fusion
  11.1 0.7 fusion.6
  11.8 2.5 %gather_fusion = bf16[160,64,128]{2,1,0:T(8,128)(2,1)} fusion(bf16[64,32,128]{2,0,1:T(8,128)(2,1)S(1)} %fusion.6, s32[1024]{0:T(1024)S(1)} %pad_clamp_fusion), kind=kCustom, calls=%fused_computation | custom fusion | bytes 5243520 | tf_op jit(solution)/shard_map/jit(_take)/gather | solution.py:105
  14.4 5.0 %copy.24 = bf16[64,160,128]{2,1,0:T(8,128)(2,1)} copy(bf16[64,160,128]{2,0,1:T(8,128)(2,1)} %bitcast.47) | data formatting | bytes 5242880 | tf_op jit(solution)/shard_map/jit(_take)/gather | solution.py:105
  19.3 0.0 copy-start.4
  19.3 4.9 %gather.7 = bf16[64,8,2560]{2,1,0:T(8,128)(2,1)S(1)} reshape(bf16[64,160,128]{2,1,0:T(8,128)(2,1)} %copy.24) | data formatting | bytes 5242880 | tf_op jit(solution)/shard_map/jit(_take)/gather | solution.py:105
  24.3 0.0 copy-done.4
  24.3 0.1 broadcast_bitcast_fusion
  24.4 1.8 select_select_fusion
  26.2 57.7 %all-gather.6.cloned.1.call-done = bf16[1,160,128,128]{3,2,0,1:T(8,128)(2,1)} async-done(((bf16[1,5,128,128]{3,2,0,1:T(8,128)(2,1)}), bf16[1,160,128,128]{3,2,0,1:T(8,128)(2,1)}) %all-gather.6.cloned.1.call-update) | async-done | bytes 5242896 | tf_op jit(solution)/shard_map/all_gather | solution.py:104
  83.9 0.0 copy-start.2
  83.9 0.0 copy-start.1
  83.9 5.1 %fusion.2 = bf16[8,64,128]{2,1,0:T(8,128)(2,1)S(1)} fusion(bf16[8,2560,128]{2,1,0:T(8,128)(2,1)} %bitcast.46, bf16[64,8,2560]{2,1,0:T(8,128)(2,1)} %select_select_fusion), kind=kOutput, calls=%fused_computation.4 | convolution fusion | flops 335609856 | bytes 7995392 | tf_op jit(solution)/shard_map/rpk,pkn->rpn/dot_general | solution.py:106
  89.1 0.0 copy-done.2
  89.1 0.7 pad_maximum_fusion.1
  89.7 0.0 all-gather.4.cloned.1.call-update
  89.8 0.1 add_select_fusion
  89.9 0.1 select_n.54.pos_ref
  90.0 68.1 %all-gather.4.cloned.1.call-done.k_ref.v_ref = bf16[2560,1024]{1,0:T(8,128)(2,1)} async-done(((bf16[80,1024]{1,0:T(8,128)(2,1)}), bf16[2560,1024]{1,0:T(8,128)(2,1)}) %all-gather.4.cloned.1.call-update) | async-done | bytes 5242896 | tf_op jit(solution)/shard_map/all_gather | solution.py:113
  158.1 0.0 copy-done.1
  158.1 3.8 %shard_map.86 = bf16[64,1024]{1,0:T(8,128)(2,1)S(1)} custom-call(s32[1]{0:T(128)} %bitcast.first_ref, s32[1,2560]{1,0:T(1,128)S(1)} %select_n.54.pos_ref, bf16[64,4096]{1,0:T(8,128)(2,1)S(1)} %bitcast.38, bf16[64,4096]{1,0:T(8,128)(2,1)S(1)} %bitcast.34, bf16[2560,1024]{1,0:T(8,128)(2,1)} %all-gather.4.cloned.1.call-done.k_ref.v_ref, ...), custom_call_target="tpu_custom_call" | custom-call | flops 671088640 | bytes 1703936 | tf_op jit(solution)/shard_map/pallas_call | solution.py:74
  161.9 3.3 %collective-permute-start = (bf16[1,64,1024]{2,1,0:T(8,128)(2,1)S(1)}, bf16[1,64,1024]{2,1,0:T(8,128)(2,1)S(1)}, u32[]{:S(2)}, u32[]{:S(2)}) collective-permute-start(bf16[1,64,1024]{2,1,0:T(8,128)(2,1)S(1)} %bitcast.42), channel_id=1, source_target_pairs={{480,0},{0,32},{32,64},{64,96},{96,128},{128,160},{160,192},{192,2... | collective-permute-start | bytes 393224 | tf_op jit(solution)/shard_map/ppermute | solution.py:19
  165.2 3.8 %shard_map.87 = bf16[64,1024]{1,0:T(8,128)(2,1)S(1)} custom-call(s32[1]{0:T(128)} %bitcast.first_ref, s32[1,2560]{1,0:T(1,128)S(1)} %select_n.54.pos_ref, bf16[64,4096]{1,0:T(8,128)(2,1)S(1)} %bitcast.39, bf16[64,4096]{1,0:T(8,128)(2,1)S(1)} %bitcast.35, bf16[2560,1024]{1,0:T(8,128)(2,1)} %all-gather.4.cloned.1.call-done.k_ref.v_ref, ...), custom_call_target="tpu_custom_call" | custom-call | flops 671088640 | bytes 1703936 | tf_op jit(solution)/shard_map/pallas_call | solution.py:74
  169.0 3.1 %collective-permute-start.1 = (bf16[1,64,1024]{2,1,0:T(8,128)(2,1)S(1)}, bf16[1,64,1024]{2,1,0:T(8,128)(2,1)S(1)}, u32[]{:S(2)}, u32[]{:S(2)}) collective-permute-start(bf16[1,64,1024]{2,1,0:T(8,128)(2,1)S(1)} %bitcast.43), channel_id=1, source_target_pairs={{480,0},{0,32},{32,64},{64,96},{96,128},{128,160},{160,192},{192,2... | collective-permute-start | bytes 393224 | tf_op jit(solution)/shard_map/ppermute | solution.py:19
  172.1 3.8 %shard_map.88 = bf16[64,1024]{1,0:T(8,128)(2,1)S(1)} custom-call(s32[1]{0:T(128)} %bitcast.first_ref, s32[1,2560]{1,0:T(1,128)S(1)} %select_n.54.pos_ref, bf16[64,4096]{1,0:T(8,128)(2,1)S(1)} %bitcast.40, bf16[64,4096]{1,0:T(8,128)(2,1)S(1)} %bitcast.36, bf16[2560,1024]{1,0:T(8,128)(2,1)} %all-gather.4.cloned.1.call-done.k_ref.v_ref, ...), custom_call_target="tpu_custom_call" | custom-call | flops 671088640 | bytes 1703936 | tf_op jit(solution)/shard_map/pallas_call | solution.py:74
  175.9 2.8 %collective-permute-start.2 = (bf16[1,64,1024]{2,1,0:T(8,128)(2,1)S(1)}, bf16[1,64,1024]{2,1,0:T(8,128)(2,1)S(1)}, u32[]{:S(2)}, u32[]{:S(2)}) collective-permute-start(bf16[1,64,1024]{2,1,0:T(8,128)(2,1)S(1)} %bitcast.44), channel_id=1, source_target_pairs={{480,0},{0,32},{32,64},{64,96},{96,128},{128,160},{160,192},{192,2... | collective-permute-start | bytes 393224 | tf_op jit(solution)/shard_map/ppermute | solution.py:19
  178.7 3.8 %shard_map.89 = bf16[64,1024]{1,0:T(8,128)(2,1)S(1)} custom-call(s32[1]{0:T(128)} %bitcast.first_ref, s32[1,2560]{1,0:T(1,128)S(1)} %select_n.54.pos_ref, bf16[64,4096]{1,0:T(8,128)(2,1)S(1)} %bitcast.41, bf16[64,4096]{1,0:T(8,128)(2,1)S(1)} %bitcast.37, bf16[2560,1024]{1,0:T(8,128)(2,1)} %all-gather.4.cloned.1.call-done.k_ref.v_ref, ...), custom_call_target="tpu_custom_call" | custom-call | flops 671088640 | bytes 1703936 | tf_op jit(solution)/shard_map/pallas_call | solution.py:74
  182.5 7.3 %collective-permute-start.3 = (bf16[1,64,1024]{2,1,0:T(8,128)(2,1)S(1)}, bf16[1,64,1024]{2,1,0:T(8,128)(2,1)S(1)}, u32[]{:S(2)}, u32[]{:S(2)}) collective-permute-start(bf16[1,64,1024]{2,1,0:T(8,128)(2,1)S(1)} %bitcast.45), channel_id=1, source_target_pairs={{480,0},{0,32},{32,64},{64,96},{96,128},{128,160},{160,192},{192,2... | collective-permute-start | bytes 393224 | tf_op jit(solution)/shard_map/ppermute | solution.py:19
  189.8 0.1 copy.27
  189.9 0.7 convert_element_type.44
  190.7 0.0 collective-permute-done
  190.7 3.9 %collective-permute-done.1 = bf16[1,64,1024]{2,1,0:T(8,128)(2,1)S(1)} collective-permute-done((bf16[1,64,1024]{2,1,0:T(8,128)(2,1)S(1)}, bf16[1,64,1024]{2,1,0:T(8,128)(2,1)S(1)}, u32[]{:S(2)}, u32[]{:S(2)}) %collective-permute-start.1) | collective-permute-done | bytes 131104 | tf_op jit(solution)/shard_map/ppermute | solution.py:19
  194.6 19.7 %collective-permute-done.2 = bf16[1,64,1024]{2,1,0:T(8,128)(2,1)S(1)} collective-permute-done((bf16[1,64,1024]{2,1,0:T(8,128)(2,1)S(1)}, bf16[1,64,1024]{2,1,0:T(8,128)(2,1)S(1)}, u32[]{:S(2)}, u32[]{:S(2)}) %collective-permute-start.2) | collective-permute-done | bytes 131104 | tf_op jit(solution)/shard_map/ppermute | solution.py:19
  214.3 5.8 %collective-permute-done.3 = bf16[1,64,1024]{2,1,0:T(8,128)(2,1)S(1)} collective-permute-done((bf16[1,64,1024]{2,1,0:T(8,128)(2,1)S(1)}, bf16[1,64,1024]{2,1,0:T(8,128)(2,1)S(1)}, u32[]{:S(2)}, u32[]{:S(2)}) %collective-permute-start.3) | collective-permute-done | bytes 131104 | tf_op jit(solution)/shard_map/ppermute | solution.py:19
  220.0 0.8 pad_maximum_fusion
  (8 shorter events, 0.1 us)
Async XLA Ops:
  7.2 3.7 %copy-start = (bf16[1,64,4096]{2,1,0:T(8,128)(2,1)S(1)}, bf16[1,64,4096]{2,1,0:T(8,128)(2,1)}, u32[]{:S(2)}) copy-start(bf16[1,64,4096]{2,1,0:T(8,128)(2,1)} %param.7) | copy-start | bytes 1572868
  7.2 3.7 %copy-start.3 = (bf16[1,4096]{1,0:T(2,128)(2,1)S(1)}, bf16[1,4096]{1,0:T(2,128)(2,1)}, u32[]{:S(2)}) copy-start(bf16[1,4096]{1,0:T(2,128)(2,1)} %param.8) | copy-start | bytes 24580
  7.2 76.7 %all-gather.6.cloned.1.call-start = ((), (), s32[]{:S(2)}) async-start(), calls=%async_computation.1 | async-start | bytes 5406720 | tf_op jit(solution)/shard_map/all_gather | solution.py:104
  7.9 150.1 %all-gather.4.cloned.1.call-start = ((), (), s32[]{:S(2)}) async-start(), calls=%async_computation | async-start | bytes 5406720 | tf_op jit(solution)/shard_map/all_gather | solution.py:113
  19.3 4.9 %copy-start.4 = (s32[1,8]{1,0:T(1,128)S(1)}, s32[1,8]{1,0:T(1,128)}, u32[]{:S(2)}) copy-start(s32[1,8]{1,0:T(1,128)} %param.13) | copy-start | bytes 100
  83.9 5.2 %copy-start.2 = (bf16[1,16,1024]{2,1,0:T(8,128)(2,1)S(1)}, bf16[1,16,1024]{2,1,0:T(8,128)(2,1)}, u32[]{:S(2)}) copy-start(bf16[1,16,1024]{2,1,0:T(8,128)(2,1)} %param.10) | copy-start | bytes 98308
  83.9 74.2 %copy-start.1 = (bf16[1,64,4096]{2,1,0:T(8,128)(2,1)S(1)}, bf16[1,64,4096]{2,1,0:T(8,128)(2,1)}, u32[]{:S(2)}) copy-start(bf16[1,64,4096]{2,1,0:T(8,128)(2,1)} %param.9) | copy-start | bytes 1572868
  161.9 28.8 %collective-permute-start = (bf16[1,64,1024]{2,1,0:T(8,128)(2,1)S(1)}, bf16[1,64,1024]{2,1,0:T(8,128)(2,1)S(1)}, u32[]{:S(2)}, u32[]{:S(2)}) collective-permute-start(bf16[1,64,1024]{2,1,0:T(8,128)(2,1)S(1)} %bitcast.42), channel_id=1, source_target_pairs={{480,0},{0,32},{32,64},{64,96},{96,128},{128,160},{160,192},{192,2... | collective-permute-start | bytes 393224 | tf_op jit(solution)/shard_map/ppermute | solution.py:19
  169.0 25.6 %collective-permute-start.1 = (bf16[1,64,1024]{2,1,0:T(8,128)(2,1)S(1)}, bf16[1,64,1024]{2,1,0:T(8,128)(2,1)S(1)}, u32[]{:S(2)}, u32[]{:S(2)}) collective-permute-start(bf16[1,64,1024]{2,1,0:T(8,128)(2,1)S(1)} %bitcast.43), channel_id=1, source_target_pairs={{480,0},{0,32},{32,64},{64,96},{96,128},{128,160},{160,192},{192,2... | collective-permute-start | bytes 393224 | tf_op jit(solution)/shard_map/ppermute | solution.py:19
  175.9 38.4 %collective-permute-start.2 = (bf16[1,64,1024]{2,1,0:T(8,128)(2,1)S(1)}, bf16[1,64,1024]{2,1,0:T(8,128)(2,1)S(1)}, u32[]{:S(2)}, u32[]{:S(2)}) collective-permute-start(bf16[1,64,1024]{2,1,0:T(8,128)(2,1)S(1)} %bitcast.44), channel_id=1, source_target_pairs={{480,0},{0,32},{32,64},{64,96},{96,128},{128,160},{160,192},{192,2... | collective-permute-start | bytes 393224 | tf_op jit(solution)/shard_map/ppermute | solution.py:19
  182.5 37.5 %collective-permute-start.3 = (bf16[1,64,1024]{2,1,0:T(8,128)(2,1)S(1)}, bf16[1,64,1024]{2,1,0:T(8,128)(2,1)S(1)}, u32[]{:S(2)}, u32[]{:S(2)}) collective-permute-start(bf16[1,64,1024]{2,1,0:T(8,128)(2,1)S(1)} %bitcast.45), channel_id=1, source_target_pairs={{480,0},{0,32},{32,64},{64,96},{96,128},{128,160},{160,192},{192,2... | collective-permute-start | bytes 393224 | tf_op jit(solution)/shard_map/ppermute | solution.py:19
Sparse Core Ops, SparseCore 0:
  10.1 73.6 all-gather.5
  89.9 68.1 all-gather.3

commit v5 on v4

--- a/solution.py
+++ b/solution.py
@@ -53,33 +53,32 @@
             ).astype(o_ref.dtype)
 
 
-def attend_group(group, first_query, key_pos, queries, residual, every_kv):
+def attend(first_query, key_pos, queries, residual, every_kv):
     rows, width = queries.shape
     key_count, kv_width = every_kv.shape
     kv_heads = kv_width // (2 * HD)
     group_width = width // kv_heads
-    heads = group_width // HD
     grid_spec = pltpu.PrefetchScalarGridSpec(
         num_scalar_prefetch=1,
-        grid=(1,),
+        grid=(kv_heads,),
         in_specs=[
-            pl.BlockSpec((1, key_count), lambda i, f: (0, 0)),
-            pl.BlockSpec((rows, group_width), lambda i, f: (0, group)),
-            pl.BlockSpec((rows, group_width), lambda i, f: (0, group)),
-            pl.BlockSpec((key_count, HD), lambda i, f: (0, group)),
-            pl.BlockSpec((key_count, HD), lambda i, f: (0, kv_heads + group)),
+            pl.BlockSpec((1, key_count), lambda g, f: (0, 0)),
+            pl.BlockSpec((rows, group_width), lambda g, f: (0, g)),
+            pl.BlockSpec((rows, group_width), lambda g, f: (0, g)),
+            pl.BlockSpec((key_count, HD), lambda g, f: (0, g)),
+            pl.BlockSpec((key_count, HD), lambda g, f: (0, kv_heads + g)),
         ],
-        out_specs=pl.BlockSpec((rows, group_width), lambda i, f: (0, 0)),
+        out_specs=pl.BlockSpec((rows, group_width), lambda g, f: (0, g)),
     )
     return pl.pallas_call(
         functools.partial(attend_kernel, stack=4),
         grid_spec=grid_spec,
-        out_shape=jax.ShapeDtypeStruct((rows, group_width), jnp.bfloat16),
+        out_shape=jax.ShapeDtypeStruct((rows, width), jnp.bfloat16),
         compiler_params=pltpu.CompilerParams(vmem_limit_bytes=48 * 1024 * 1024),
         cost_estimate=pl.CostEstimate(
-            flops=4 * rows * heads * key_count * HD,
-            transcendentals=rows * heads * key_count,
-            bytes_accessed=2 * (3 * rows * group_width + 2 * key_count * HD),
+            flops=4 * rows * (width // HD) * key_count * HD,
+            transcendentals=rows * (width // HD) * key_count,
+            bytes_accessed=2 * (3 * rows * width + key_count * kv_width),
         ),
     )(first_query.reshape(1).astype(jnp.int32), key_pos, queries, residual, every_kv, every_kv)
 
@@ -120,17 +119,8 @@
         -1,
     ).reshape(1, -1)
     first_query = zero_index * row_count
-    passed = jnp.concatenate(
-        [
-            passed_along(
-                attend_group(group, first_query, key_pos, queries[0], residual[0], every_kv)[None],
-                "pipe",
-                1,
-            )
-            for group in range(cached_kv.shape[2] // (2 * HD))
-        ],
-        axis=-1,
-    )
+    updated = attend(first_query, key_pos, queries[0], residual[0], every_kv)
+    passed = passed_along(updated[None], "pipe", 1)
     return (passed, kv_new[None])
 
 

time: 228 us -> 231 us (1.013)
  the two profiles are of different devices: /device:TPU:3 before, /device:TPU:96 now
where the time goes in v5:
time: 231 us; the launch traced here: 230 us
  waiting for transfers between devices  175 us (76%)
  local copies, waits for them, and re-layouts  15.3 us (7%)
  between operations  14.2 us (6%)
  Pallas kernels  11.4 us (5%)
  other arithmetic  5.3 us (2%)
  matrix products  5.15 us (2%)
  starting transfers between devices  3.47 us (2%)
    all_gather x1, waiting for transfers between devices, local(): lax.all_gather(jnp.concatenate([kv_new, cached_kv[0]], axis=0), 'zero', a...  67.9 us
    all_gather x1, waiting for transfers between devices, local(): every_block = lax.all_gather(panel_blocks[0], 'zero', axis=0, tiled=True)  55.1 us
    ppermute x1, waiting for transfers between devices, passed_along(): return lax.ppermute(block, axis, route)  51.6 us
    gather x3, local copies, waits for them, and re-layouts, local(): jnp.take(normed_grid, row_table, axis=1)  12.4 us
    pallas_call x1, Pallas kernels, attend(): pl.pallas_call(functools.partial(attend_kernel, stack=4), grid_spec=grid_...  11.4 us
    dot_general x1, matrix products, local(): jnp.einsum('rpk,pkn->rpn', chosen.reshape(row_count, panels, slot_depth *...  5.15 us
  transfers between devices with their start and end apart: 3, of which 3 were waited for; matrix products, arithmetic and copies ran while one was open for 8% of the time, Pallas kernels for 0%

profile of v5, /device:TPU:96, one launch (start us, length us, event | category | flops | bytes accessed | tf_op | source)
XLA Modules:
  0.0 230.1 jit_solution(13904284417342671313)
XLA Ops:
  7.2 0.0 copy-start
  7.2 0.0 copy-start.3
  7.2 0.0 all-gather.6.cloned.1.call-start
  7.2 0.7 all-gather.6.cloned.1.call-update
  7.9 0.0 all-gather.4.cloned.1.call-start
  8.0 0.8 reshape_squeeze.6
  8.7 0.7 compare_and_fusion
  9.4 0.1 copy.22
  9.5 1.1 convert_bitcast_fusion
  10.6 0.2 copy.30
  10.8 0.0 copy-done.3
  10.9 0.0 copy-done
  10.9 0.2 multiply_reduce_fusion
  11.1 0.7 fusion.6
  11.8 2.5 %gather_fusion = bf16[160,64,128]{2,1,0:T(8,128)(2,1)} fusion(bf16[64,32,128]{2,0,1:T(8,128)(2,1)S(1)} %fusion.6, s32[1024]{0:T(1024)S(1)} %pad_clamp_fusion), kind=kCustom, calls=%fused_computation | custom fusion | bytes 5243520 | tf_op jit(solution)/shard_map/jit(_take)/gather | solution.py:104
  14.4 5.0 %copy.24 = bf16[64,160,128]{2,1,0:T(8,128)(2,1)} copy(bf16[64,160,128]{2,0,1:T(8,128)(2,1)} %bitcast.35) | data formatting | bytes 5242880 | tf_op jit(solution)/shard_map/jit(_take)/gather | solution.py:104
  19.3 0.0 copy-start.4
  19.3 4.9 %gather.7 = bf16[64,8,2560]{2,1,0:T(8,128)(2,1)S(1)} reshape(bf16[64,160,128]{2,1,0:T(8,128)(2,1)} %copy.24) | data formatting | bytes 5242880 | tf_op jit(solution)/shard_map/jit(_take)/gather | solution.py:104
  24.3 0.0 copy-done.4
  24.3 0.1 broadcast_bitcast_fusion
  24.4 1.8 select_select_fusion
  26.2 55.1 %all-gather.6.cloned.1.call-done = bf16[1,160,128,128]{3,2,0,1:T(8,128)(2,1)} async-done(((bf16[1,5,128,128]{3,2,0,1:T(8,128)(2,1)}), bf16[1,160,128,128]{3,2,0,1:T(8,128)(2,1)}) %all-gather.6.cloned.1.call-update) | async-done | bytes 5242896 | tf_op jit(solution)/shard_map/all_gather | solution.py:103
  81.3 0.0 copy-start.2
  81.3 0.0 copy-start.1
  81.3 5.1 %fusion.2 = bf16[8,64,128]{2,1,0:T(8,128)(2,1)S(1)} fusion(bf16[8,2560,128]{2,1,0:T(8,128)(2,1)} %bitcast.34, bf16[64,8,2560]{2,1,0:T(8,128)(2,1)} %select_select_fusion), kind=kOutput, calls=%fused_computation.4 | convolution fusion | flops 335609856 | bytes 7995392 | tf_op jit(solution)/shard_map/rpk,pkn->rpn/dot_general | solution.py:105
  86.5 0.0 copy-done.2
  86.5 0.7 pad_maximum_fusion
  87.1 0.0 all-gather.4.cloned.1.call-update
  87.2 0.1 add_select_fusion
  87.3 0.1 select_n.42.pos_ref
  87.4 67.9 %all-gather.4.cloned.1.call-done.k_ref.v_ref = bf16[2560,1024]{1,0:T(8,128)(2,1)} async-done(((bf16[80,1024]{1,0:T(8,128)(2,1)}), bf16[2560,1024]{1,0:T(8,128)(2,1)}) %all-gather.4.cloned.1.call-update) | async-done | bytes 5242896 | tf_op jit(solution)/shard_map/all_gather | solution.py:112
  155.3 0.0 copy-done.1
  155.3 11.4 %shard_map.86 = bf16[64,4096]{1,0:T(8,128)(2,1)S(1)} custom-call(s32[1]{0:T(128)} %bitcast.first_ref, s32[1,2560]{1,0:T(1,128)S(1)} %select_n.42.pos_ref, bf16[64,4096]{1,0:T(8,128)(2,1)S(1)} %bitcast.32, bf16[64,4096]{1,0:T(8,128)(2,1)S(1)} %bitcast.31, bf16[2560,1024]{1,0:T(8,128)(2,1)} %all-gather.4.cloned.1.call-done.k_ref.v_ref, ...), custom_call_target="tpu_custom_call" | custom-call | flops 2684354560 | bytes 6815744 | tf_op jit(solution)/shard_map/pallas_call | solution.py:73
  166.7 3.4 %collective-permute-start = (bf16[1,64,4096]{2,1,0:T(8,128)(2,1)S(1)}, bf16[1,64,4096]{2,1,0:T(8,128)(2,1)S(1)}, u32[]{:S(2)}, u32[]{:S(2)}) collective-permute-start(bf16[1,64,4096]{2,1,0:T(8,128)(2,1)S(1)} %bitcast.33), channel_id=1, source_target_pairs={{480,0},{0,32},{32,64},{64,96},{96,128},{128,160},{160,192},{192,2... | collective-permute-start | bytes 1572872 | tf_op jit(solution)/shard_map/ppermute | solution.py:19
  170.1 0.1 copy.27
  170.2 0.7 convert_element_type.44
  170.9 51.6 %collective-permute-done = bf16[1,64,4096]{2,1,0:T(8,128)(2,1)S(1)} collective-permute-done((bf16[1,64,4096]{2,1,0:T(8,128)(2,1)S(1)}, bf16[1,64,4096]{2,1,0:T(8,128)(2,1)S(1)}, u32[]{:S(2)}, u32[]{:S(2)}) %collective-permute-start) | collective-permute-done | bytes 524320 | tf_op jit(solution)/shard_map/ppermute | solution.py:19
  222.5 0.8 copy.42
  (8 shorter events, 0.1 us)
Async XLA Ops:
  7.2 3.7 %copy-start = (bf16[1,64,4096]{2,1,0:T(8,128)(2,1)S(1)}, bf16[1,64,4096]{2,1,0:T(8,128)(2,1)}, u32[]{:S(2)}) copy-start(bf16[1,64,4096]{2,1,0:T(8,128)(2,1)} %param.7) | copy-start | bytes 1572868
  7.2 3.7 %copy-start.3 = (bf16[1,4096]{1,0:T(2,128)(2,1)S(1)}, bf16[1,4096]{1,0:T(2,128)(2,1)}, u32[]{:S(2)}) copy-start(bf16[1,4096]{1,0:T(2,128)(2,1)} %param.8) | copy-start | bytes 24580
  7.2 74.1 %all-gather.6.cloned.1.call-start = ((), (), s32[]{:S(2)}) async-start(), calls=%async_computation.1 | async-start | bytes 5406720 | tf_op jit(solution)/shard_map/all_gather | solution.py:103
  7.9 147.4 %all-gather.4.cloned.1.call-start = ((), (), s32[]{:S(2)}) async-start(), calls=%async_computation | async-start | bytes 5406720 | tf_op jit(solution)/shard_map/all_gather | solution.py:112
  19.3 4.9 %copy-start.4 = (s32[1,8]{1,0:T(1,128)S(1)}, s32[1,8]{1,0:T(1,128)}, u32[]{:S(2)}) copy-start(s32[1,8]{1,0:T(1,128)} %param.13) | copy-start | bytes 100
  81.3 5.2 %copy-start.2 = (bf16[1,16,1024]{2,1,0:T(8,128)(2,1)S(1)}, bf16[1,16,1024]{2,1,0:T(8,128)(2,1)}, u32[]{:S(2)}) copy-start(bf16[1,16,1024]{2,1,0:T(8,128)(2,1)} %param.10) | copy-start | bytes 98308
  81.3 74.0 %copy-start.1 = (bf16[1,64,4096]{2,1,0:T(8,128)(2,1)S(1)}, bf16[1,64,4096]{2,1,0:T(8,128)(2,1)}, u32[]{:S(2)}) copy-start(bf16[1,64,4096]{2,1,0:T(8,128)(2,1)} %param.9) | copy-start | bytes 1572868
  166.7 55.8 %collective-permute-start = (bf16[1,64,4096]{2,1,0:T(8,128)(2,1)S(1)}, bf16[1,64,4096]{2,1,0:T(8,128)(2,1)S(1)}, u32[]{:S(2)}, u32[]{:S(2)}) collective-permute-start(bf16[1,64,4096]{2,1,0:T(8,128)(2,1)S(1)} %bitcast.33), channel_id=1, source_target_pairs={{480,0},{0,32},{32,64},{64,96},{96,128},{128,160},{160,192},{192,2... | collective-permute-start | bytes 1572872 | tf_op jit(solution)/shard_map/ppermute | solution.py:19
Sparse Core Ops, SparseCore 0:
  10.1 71.0 all-gather.5
  87.3 67.9 all-gather.3

commit v6 on v5

--- a/solution.py
+++ b/solution.py
@@ -11,6 +11,23 @@
 QH = 32
 KVH = 4
 HD = 128
+PIPE_SPAN = 4
+
+
+def relay_along(block, axis, span):
+    size = lax.axis_size(axis)
+    half = block.shape[-1] // 2
+    direct_half, relayed_half = block[..., :half], block[..., half:]
+    crossing = [p for p in range(size) if p % span == span - 1]
+    first = lax.ppermute(direct_half, axis, [(p, (p + 1) % size) for p in range(size)])
+    second = lax.ppermute(
+        relayed_half, axis, [(p, (p + 1) % size) for p in range(size) if p % span != span - 1]
+    )
+    leg = lax.ppermute(relayed_half, axis, [(p, p - 1) for p in crossing])
+    leg = lax.ppermute(leg, axis, [(p - 1, (p - 1 + span) % size) for p in crossing])
+    leg = lax.ppermute(leg, axis, [((p + span) % size - 1, (p + 1) % size) for p in crossing])
+    lands = lax.axis_index(axis) % span == 0
+    return jnp.concatenate([first, jnp.where(lands, leg, second)], axis=-1)
 
 
 def passed_along(block, axis, distance):
@@ -120,7 +137,7 @@
     ).reshape(1, -1)
     first_query = zero_index * row_count
     updated = attend(first_query, key_pos, queries[0], residual[0], every_kv)
-    passed = passed_along(updated[None], "pipe", 1)
+    passed = relay_along(updated[None], "pipe", PIPE_SPAN)
     return (passed, kv_new[None])
 
 

time: 231 us -> 229 us (level)
  the two profiles are of different devices: /device:TPU:96 before, /device:TPU:120 now
where the time goes in v6:
time: 229 us
  waiting for transfers between devices  170 us (74%)
  local copies, waits for them, and re-layouts  14.6 us (6%)
  between operations  14.3 us (6%)
  Pallas kernels  11.4 us (5%)
  starting transfers between devices  7.79 us (3%)
  other arithmetic  6.15 us (3%)
  matrix products  5.15 us (2%)
    all_gather x1, waiting for transfers between devices, local(): lax.all_gather(jnp.concatenate([kv_new, cached_kv[0]], axis=0), 'zero', a...  68 us
    all_gather x1, waiting for transfers between devices, local(): every_block = lax.all_gather(panel_blocks[0], 'zero', axis=0, tiled=True)  54.8 us
    ppermute x1, waiting for transfers between devices, relay_along(): lax.ppermute(direct_half, axis, [(p, (p + 1) % size) for p in range(size)])  28.4 us
    gather x3, local copies, waits for them, and re-layouts, local(): jnp.take(normed_grid, row_table, axis=1)  12.4 us
    ppermute x1, waiting for transfers between devices, relay_along(): lax.ppermute(relayed_half, axis, [(p, (p + 1) % size) for p in range(size...  11.6 us
    pallas_call x1, Pallas kernels, attend(): pl.pallas_call(functools.partial(attend_kernel, stack=4), grid_spec=grid_...  11.4 us
    ppermute x1, waiting for transfers between devices, relay_along(): leg = lax.ppermute(relayed_half, axis, [(p, p - 1) for p in crossing])  5.92 us
    dot_general x1, matrix products, local(): jnp.einsum('rpk,pkn->rpn', chosen.reshape(row_count, panels, slot_depth *...  5.15 us
  transfers between devices with their start and end apart: 7, of which 5 were waited for; matrix products, arithmetic and copies ran while one was open for 8% of the time, Pallas kernels for 0%

profile of v6, /device:TPU:120, one launch (start us, length us, event | category | flops | bytes accessed | tf_op | source)
XLA Modules:
  0.0 228.9 jit_solution(4866492318512954160)
XLA Ops:
  7.2 0.0 copy-start
  7.2 0.0 copy-start.3
  7.2 0.0 all-gather.6.cloned.1.call-start
  7.2 0.7 all-gather.6.cloned.1.call-update
  7.9 0.0 all-gather.4.cloned.1.call-start
  8.0 0.8 reshape_squeeze.6
  8.7 0.7 compare_and_fusion
  9.4 0.1 copy.22
  9.5 1.1 convert_bitcast_fusion
  10.6 0.2 copy.30
  10.8 0.0 copy-done.3
  10.9 0.0 copy-done
  10.9 0.2 multiply_reduce_fusion
  11.1 0.7 fusion.6
  11.8 2.5 %gather_fusion = bf16[160,64,128]{2,1,0:T(8,128)(2,1)} fusion(bf16[64,32,128]{2,0,1:T(8,128)(2,1)S(1)} %fusion.6, s32[1024]{0:T(1024)S(1)} %pad_clamp_fusion), kind=kCustom, calls=%fused_computation | custom fusion | bytes 5243520 | tf_op jit(solution)/shard_map/jit(_take)/gather | solution.py:121
  14.3 5.0 %copy.24 = bf16[64,160,128]{2,1,0:T(8,128)(2,1)} copy(bf16[64,160,128]{2,0,1:T(8,128)(2,1)} %bitcast.35) | data formatting | bytes 5242880 | tf_op jit(solution)/shard_map/jit(_take)/gather | solution.py:121
  19.3 0.0 copy-start.4
  19.3 4.9 %gather.7 = bf16[64,8,2560]{2,1,0:T(8,128)(2,1)S(1)} reshape(bf16[64,160,128]{2,1,0:T(8,128)(2,1)} %copy.24) | data formatting | bytes 5242880 | tf_op jit(solution)/shard_map/jit(_take)/gather | solution.py:121
  24.3 0.0 copy-done.4
  24.3 0.1 broadcast_bitcast_fusion
  24.4 1.8 select_select_fusion
  26.2 54.8 %all-gather.6.cloned.1.call-done = bf16[1,160,128,128]{3,2,0,1:T(8,128)(2,1)} async-done(((bf16[1,5,128,128]{3,2,0,1:T(8,128)(2,1)}), bf16[1,160,128,128]{3,2,0,1:T(8,128)(2,1)}) %all-gather.6.cloned.1.call-update) | async-done | bytes 5242896 | tf_op jit(solution)/shard_map/all_gather | solution.py:120
  81.0 0.0 copy-start.2
  81.0 0.0 copy-start.1
  81.0 5.1 %fusion.2 = bf16[8,64,128]{2,1,0:T(8,128)(2,1)S(1)} fusion(bf16[8,2560,128]{2,1,0:T(8,128)(2,1)} %bitcast.34, bf16[64,8,2560]{2,1,0:T(8,128)(2,1)} %select_select_fusion), kind=kOutput, calls=%fused_computation.4 | convolution fusion | flops 335609856 | bytes 7995392 | tf_op jit(solution)/shard_map/rpk,pkn->rpn/dot_general | solution.py:122
  86.2 0.0 copy-done.2
  86.2 0.7 pad_maximum_fusion.1
  86.9 0.0 all-gather.4.cloned.1.call-update
  86.9 0.1 add_select_fusion
  87.0 0.1 select_n.57.pos_ref
  87.1 68.0 %all-gather.4.cloned.1.call-done.k_ref.v_ref = bf16[2560,1024]{1,0:T(8,128)(2,1)} async-done(((bf16[80,1024]{1,0:T(8,128)(2,1)}), bf16[2560,1024]{1,0:T(8,128)(2,1)}) %all-gather.4.cloned.1.call-update) | async-done | bytes 5242896 | tf_op jit(solution)/shard_map/all_gather | solution.py:129
  155.1 0.0 copy-done.1
  155.1 11.4 %shard_map.86 = bf16[64,4096]{1,0:T(8,128)(2,1)S(1)} custom-call(s32[1]{0:T(128)} %bitcast.first_ref, s32[1,2560]{1,0:T(1,128)S(1)} %select_n.57.pos_ref, bf16[64,4096]{1,0:T(8,128)(2,1)S(1)} %bitcast.33, bf16[64,4096]{1,0:T(8,128)(2,1)S(1)} %bitcast.31, bf16[2560,1024]{1,0:T(8,128)(2,1)} %all-gather.4.cloned.1.call-done.k_ref.v_ref, ...), custom_call_target="tpu_custom_call" | custom-call | flops 2684354560 | bytes 6815744 | tf_op jit(solution)/shard_map/pallas_call | solution.py:90
  166.6 2.7 %collective-permute-start.1 = (bf16[1,64,2048]{2,1,0:T(8,128)(2,1)S(1)}, bf16[1,64,2048]{2,1,0:T(8,128)(2,1)S(1)}, u32[]{:S(2)}, u32[]{:S(2)}) collective-permute-start(bf16[1,64,2048]{2,1,0:T(8,128)(2,1)S(1)} %get-tuple-element.3), channel_id=1, source_target_pairs={{96,64},{224,192},{352,320},{480,448},{97,65},{225,193},{353,321},... | collective-permute-start | bytes 786440 | tf_op jit(solution)/shard_map/ppermute | solution.py:26
  169.3 5.9 %collective-permute-done.1 = bf16[1,64,2048]{2,1,0:T(8,128)(2,1)S(1)} collective-permute-done((bf16[1,64,2048]{2,1,0:T(8,128)(2,1)S(1)}, bf16[1,64,2048]{2,1,0:T(8,128)(2,1)S(1)}, u32[]{:S(2)}, u32[]{:S(2)}) %collective-permute-start.1) | collective-permute-done | bytes 262176 | tf_op jit(solution)/shard_map/ppermute | solution.py:26
  175.2 0.7 collective-permute-start.2
  175.9 1.3 collective-permute-start.4
  177.2 0.0 collective-permute-done.2
  177.2 0.7 collective-permute-start.3
  177.9 0.1 copy.27
  178.0 0.7 convert_element_type.44
  178.7 2.4 %collective-permute-start = (bf16[1,64,2048]{2,1,0:T(8,128)(2,1)S(1)}, bf16[1,64,2048]{2,1,0:T(8,128)(2,1)S(1)}, u32[]{:S(2)}, u32[]{:S(2)}) collective-permute-start(bf16[1,64,2048]{2,1,0:T(8,128)(2,1)S(1)} %get-tuple-element.2), channel_id=1, source_target_pairs={{0,32},{32,64},{64,96},{96,128},{128,160},{160,192},{192,224},{224... | collective-permute-start | bytes 786440 | tf_op jit(solution)/shard_map/ppermute | solution.py:22
  181.1 11.6 %collective-permute-done.4 = bf16[1,64,2048]{2,1,0:T(8,128)(2,1)S(1)} collective-permute-done((bf16[1,64,2048]{2,1,0:T(8,128)(2,1)S(1)}, bf16[1,64,2048]{2,1,0:T(8,128)(2,1)S(1)}, u32[]{:S(2)}, u32[]{:S(2)}) %collective-permute-start.4) | collective-permute-done | bytes 262176 | tf_op jit(solution)/shard_map/ppermute | solution.py:23
  192.8 0.0 collective-permute-done.3
  192.8 28.4 %collective-permute-done = bf16[1,64,2048]{2,1,0:T(8,128)(2,1)S(1)} collective-permute-done((bf16[1,64,2048]{2,1,0:T(8,128)(2,1)S(1)}, bf16[1,64,2048]{2,1,0:T(8,128)(2,1)S(1)}, u32[]{:S(2)}, u32[]{:S(2)}) %collective-permute-start) | collective-permute-done | bytes 262176 | tf_op jit(solution)/shard_map/ppermute | solution.py:22
  221.2 0.8 pad_maximum_fusion
  (10 shorter events, 0.1 us)
Async XLA Ops:
  7.2 3.7 %copy-start = (bf16[1,64,4096]{2,1,0:T(8,128)(2,1)S(1)}, bf16[1,64,4096]{2,1,0:T(8,128)(2,1)}, u32[]{:S(2)}) copy-start(bf16[1,64,4096]{2,1,0:T(8,128)(2,1)} %param.7) | copy-start | bytes 1572868
  7.2 3.7 %copy-start.3 = (bf16[1,4096]{1,0:T(2,128)(2,1)S(1)}, bf16[1,4096]{1,0:T(2,128)(2,1)}, u32[]{:S(2)}) copy-start(bf16[1,4096]{1,0:T(2,128)(2,1)} %param.8) | copy-start | bytes 24580
  7.2 73.8 %all-gather.6.cloned.1.call-start = ((), (), s32[]{:S(2)}) async-start(), calls=%async_computation.1 | async-start | bytes 5406720 | tf_op jit(solution)/shard_map/all_gather | solution.py:120
  7.9 147.2 %all-gather.4.cloned.1.call-start = ((), (), s32[]{:S(2)}) async-start(), calls=%async_computation | async-start | bytes 5406720 | tf_op jit(solution)/shard_map/all_gather | solution.py:129
  19.3 4.9 %copy-start.4 = (s32[1,8]{1,0:T(1,128)S(1)}, s32[1,8]{1,0:T(1,128)}, u32[]{:S(2)}) copy-start(s32[1,8]{1,0:T(1,128)} %param.13) | copy-start | bytes 100
  81.0 5.2 %copy-start.2 = (bf16[1,16,1024]{2,1,0:T(8,128)(2,1)S(1)}, bf16[1,16,1024]{2,1,0:T(8,128)(2,1)}, u32[]{:S(2)}) copy-start(bf16[1,16,1024]{2,1,0:T(8,128)(2,1)} %param.10) | copy-start | bytes 98308
  81.0 74.1 %copy-start.1 = (bf16[1,64,4096]{2,1,0:T(8,128)(2,1)S(1)}, bf16[1,64,4096]{2,1,0:T(8,128)(2,1)}, u32[]{:S(2)}) copy-start(bf16[1,64,4096]{2,1,0:T(8,128)(2,1)} %param.9) | copy-start | bytes 1572868
  166.6 8.6 %collective-permute-start.1 = (bf16[1,64,2048]{2,1,0:T(8,128)(2,1)S(1)}, bf16[1,64,2048]{2,1,0:T(8,128)(2,1)S(1)}, u32[]{:S(2)}, u32[]{:S(2)}) collective-permute-start(bf16[1,64,2048]{2,1,0:T(8,128)(2,1)S(1)} %get-tuple-element.3), channel_id=1, source_target_pairs={{96,64},{224,192},{352,320},{480,448},{97,65},{225,193},{353,321},... | collective-permute-start | bytes 786440 | tf_op jit(solution)/shard_map/ppermute | solution.py:26
  175.2 2.0 collective-permute-start.2
  175.9 16.9 %collective-permute-start.4 = (bf16[1,64,2048]{2,1,0:T(8,128)(2,1)S(1)}, bf16[1,64,2048]{2,1,0:T(8,128)(2,1)S(1)}, u32[]{:S(2)}, u32[]{:S(2)}) collective-permute-start(bf16[1,64,2048]{2,1,0:T(8,128)(2,1)S(1)} %get-tuple-element.3), channel_id=1, source_target_pairs={{0,32},{32,64},{64,96},{128,160},{160,192},{192,224},{256,288},{28... | collective-permute-start | bytes 786440 | tf_op jit(solution)/shard_map/ppermute | solution.py:23
  177.2 15.6 %collective-permute-start.3 = (bf16[1,64,2048]{2,1,0:T(8,128)(2,1)S(1)}, bf16[1,64,2048]{2,1,0:T(8,128)(2,1)S(1)}, u32[]{:S(2)}, u32[]{:S(2)}) collective-permute-start(bf16[1,64,2048]{2,1,0:T(8,128)(2,1)S(1)} %collective-permute-done.2), channel_id=1, source_target_pairs={{192,128},{320,256},{448,384},{64,0},{193,129},{321,257},{449,385}... | collective-permute-start | bytes 786440 | tf_op jit(solution)/shard_map/ppermute | solution.py:28
  178.7 42.5 %collective-permute-start = (bf16[1,64,2048]{2,1,0:T(8,128)(2,1)S(1)}, bf16[1,64,2048]{2,1,0:T(8,128)(2,1)S(1)}, u32[]{:S(2)}, u32[]{:S(2)}) collective-permute-start(bf16[1,64,2048]{2,1,0:T(8,128)(2,1)S(1)} %get-tuple-element.2), channel_id=1, source_target_pairs={{0,32},{32,64},{64,96},{96,128},{128,160},{160,192},{192,224},{224... | collective-permute-start | bytes 786440 | tf_op jit(solution)/shard_map/ppermute | solution.py:22
Sparse Core Ops, SparseCore 0:
  10.1 70.8 all-gather.5
  87.0 68.0 all-gather.3

commit v7 on v6

--- a/solution.py
+++ b/solution.py
@@ -21,11 +21,12 @@
     crossing = [p for p in range(size) if p % span == span - 1]
     first = lax.ppermute(direct_half, axis, [(p, (p + 1) % size) for p in range(size)])
     second = lax.ppermute(
-        relayed_half, axis, [(p, (p + 1) % size) for p in range(size) if p % span != span - 1]
+        relayed_half,
+        axis,
+        [(p, (p + 1) % size) for p in range(size) if p % span != span - 1]
+        + [(p, p + 1 - span) for p in crossing],
     )
-    leg = lax.ppermute(relayed_half, axis, [(p, p - 1) for p in crossing])
-    leg = lax.ppermute(leg, axis, [(p - 1, (p - 1 + span) % size) for p in crossing])
-    leg = lax.ppermute(leg, axis, [((p + span) % size - 1, (p + 1) % size) for p in crossing])
+    leg = lax.ppermute(second, axis, [(p + 1 - span, (p + 1) % size) for p in crossing])
     lands = lax.axis_index(axis) % span == 0
     return jnp.concatenate([first, jnp.where(lands, leg, second)], axis=-1)
 

time: 229 us -> 227 us (level)
  the two profiles are of different devices: /device:TPU:120 before, /device:TPU:64 now
where the time goes in v7:
time: 227 us
  waiting for transfers between devices  162 us (71%)
  local copies, waits for them, and re-layouts  14.6 us (6%)
  between operations  14.3 us (6%)
  starting transfers between devices  13 us (6%)
  Pallas kernels  11.4 us (5%)
  other arithmetic  6.14 us (3%)
  matrix products  5.15 us (2%)
    all_gather x1, waiting for transfers between devices, local(): lax.all_gather(jnp.concatenate([kv_new, cached_kv[0]], axis=0), 'zero', a...  68.1 us
    all_gather x1, waiting for transfers between devices, local(): every_block = lax.all_gather(panel_blocks[0], 'zero', axis=0, tiled=True)  55.5 us
    ppermute x1, waiting for transfers between devices, relay_along(): lax.ppermute(second, axis, [(p + 1 - span, (p + 1) % size) for p in cross...  17 us
    ppermute x1, waiting for transfers between devices, relay_along(): lax.ppermute(direct_half, axis, [(p, (p + 1) % size) for p in range(size)])  13.1 us
    gather x3, local copies, waits for them, and re-layouts, local(): jnp.take(normed_grid, row_table, axis=1)  12.4 us
    pallas_call x1, Pallas kernels, attend(): pl.pallas_call(functools.partial(attend_kernel, stack=4), grid_spec=grid_...  11.4 us
    ppermute x1, waiting for transfers between devices, relay_along(): lax.ppermute(relayed_half, axis, [(p, (p + 1) % size) for p in range(size...  8.14 us
    ppermute x1, starting transfers between devices, relay_along(): lax.ppermute(second, axis, [(p + 1 - span, (p + 1) % size) for p in cross...  7.63 us
  transfers between devices with their start and end apart: 5, of which 5 were waited for; matrix products, arithmetic and copies ran while one was open for 8% of the time, Pallas kernels for 0%

profile of v7, /device:TPU:64, one launch (start us, length us, event | category | flops | bytes accessed | tf_op | source)
XLA Modules:
  0.0 227.0 jit_solution(7150491672645070053)
XLA Ops:
  7.2 0.0 copy-start
  7.2 0.0 copy-start.3
  7.2 0.0 all-gather.6.cloned.1.call-start
  7.2 0.7 all-gather.6.cloned.1.call-update
  7.9 0.0 all-gather.4.cloned.1.call-start
  8.0 0.8 reshape_squeeze.6
  8.7 0.7 compare_and_fusion
  9.4 0.1 copy.22
  9.5 1.1 convert_bitcast_fusion
  10.6 0.2 copy.30
  10.8 0.0 copy-done.3
  10.9 0.0 copy-done
  10.9 0.2 multiply_reduce_fusion
  11.1 0.7 fusion.6
  11.8 2.5 %gather_fusion = bf16[160,64,128]{2,1,0:T(8,128)(2,1)} fusion(bf16[64,32,128]{2,0,1:T(8,128)(2,1)S(1)} %fusion.6, s32[1024]{0:T(1024)S(1)} %pad_clamp_fusion), kind=kCustom, calls=%fused_computation | custom fusion | bytes 5243520 | tf_op jit(solution)/shard_map/jit(_take)/gather | solution.py:122
  14.4 5.0 %copy.24 = bf16[64,160,128]{2,1,0:T(8,128)(2,1)} copy(bf16[64,160,128]{2,0,1:T(8,128)(2,1)} %bitcast.35) | data formatting | bytes 5242880 | tf_op jit(solution)/shard_map/jit(_take)/gather | solution.py:122
  19.3 0.0 copy-start.4
  19.3 4.9 %gather.7 = bf16[64,8,2560]{2,1,0:T(8,128)(2,1)S(1)} reshape(bf16[64,160,128]{2,1,0:T(8,128)(2,1)} %copy.24) | data formatting | bytes 5242880 | tf_op jit(solution)/shard_map/jit(_take)/gather | solution.py:122
  24.3 0.0 copy-done.4
  24.3 0.1 broadcast_bitcast_fusion
  24.4 1.8 select_select_fusion
  26.2 55.5 %all-gather.6.cloned.1.call-done = bf16[1,160,128,128]{3,2,0,1:T(8,128)(2,1)} async-done(((bf16[1,5,128,128]{3,2,0,1:T(8,128)(2,1)}), bf16[1,160,128,128]{3,2,0,1:T(8,128)(2,1)}) %all-gather.6.cloned.1.call-update) | async-done | bytes 5242896 | tf_op jit(solution)/shard_map/all_gather | solution.py:121
  81.7 0.0 copy-start.2
  81.7 0.0 copy-start.1
  81.7 5.1 %fusion.2 = bf16[8,64,128]{2,1,0:T(8,128)(2,1)S(1)} fusion(bf16[8,2560,128]{2,1,0:T(8,128)(2,1)} %bitcast.34, bf16[64,8,2560]{2,1,0:T(8,128)(2,1)} %select_select_fusion), kind=kOutput, calls=%fused_computation.4 | convolution fusion | flops 335609856 | bytes 7995392 | tf_op jit(solution)/shard_map/rpk,pkn->rpn/dot_general | solution.py:123
  86.9 0.0 copy-done.2
  86.9 0.7 pad_maximum_fusion.1
  87.6 0.0 all-gather.4.cloned.1.call-update
  87.6 0.1 add_select_fusion
  87.7 0.1 select_n.57.pos_ref
  87.8 68.1 %all-gather.4.cloned.1.call-done.k_ref.v_ref = bf16[2560,1024]{1,0:T(8,128)(2,1)} async-done(((bf16[80,1024]{1,0:T(8,128)(2,1)}), bf16[2560,1024]{1,0:T(8,128)(2,1)}) %all-gather.4.cloned.1.call-update) | async-done | bytes 5242896 | tf_op jit(solution)/shard_map/all_gather | solution.py:130
  155.8 0.0 copy-done.1
  155.8 11.4 %shard_map.86 = bf16[64,4096]{1,0:T(8,128)(2,1)S(1)} custom-call(s32[1]{0:T(128)} %bitcast.first_ref, s32[1,2560]{1,0:T(1,128)S(1)} %select_n.57.pos_ref, bf16[64,4096]{1,0:T(8,128)(2,1)S(1)} %bitcast.33, bf16[64,4096]{1,0:T(8,128)(2,1)S(1)} %bitcast.31, bf16[2560,1024]{1,0:T(8,128)(2,1)} %all-gather.4.cloned.1.call-done.k_ref.v_ref, ...), custom_call_target="tpu_custom_call" | custom-call | flops 2684354560 | bytes 6815744 | tf_op jit(solution)/shard_map/pallas_call | solution.py:91
  167.3 3.4 %collective-permute-start.1 = (bf16[1,64,2048]{2,1,0:T(8,128)(2,1)S(1)}, bf16[1,64,2048]{2,1,0:T(8,128)(2,1)S(1)}, u32[]{:S(2)}, u32[]{:S(2)}) collective-permute-start(bf16[1,64,2048]{2,1,0:T(8,128)(2,1)S(1)} %get-tuple-element.3), channel_id=1, source_target_pairs={{0,32},{32,64},{64,96},{128,160},{160,192},{192,224},{256,288},{28... | collective-permute-start | bytes 786440 | tf_op jit(solution)/shard_map/ppermute | solution.py:23
  170.7 8.1 %collective-permute-done.1 = bf16[1,64,2048]{2,1,0:T(8,128)(2,1)S(1)} collective-permute-done((bf16[1,64,2048]{2,1,0:T(8,128)(2,1)S(1)}, bf16[1,64,2048]{2,1,0:T(8,128)(2,1)S(1)}, u32[]{:S(2)}, u32[]{:S(2)}) %collective-permute-start.1) | collective-permute-done | bytes 262176 | tf_op jit(solution)/shard_map/ppermute | solution.py:23
  178.9 7.6 %collective-permute-start.2 = (bf16[1,64,2048]{2,1,0:T(8,128)(2,1)S(1)}, bf16[1,64,2048]{2,1,0:T(8,128)(2,1)S(1)}, u32[]{:S(2)}, u32[]{:S(2)}) collective-permute-start(bf16[1,64,2048]{2,1,0:T(8,128)(2,1)S(1)} %collective-permute-done.1), channel_id=1, source_target_pairs={{0,128},{128,256},{256,384},{384,0},{1,129},{129,257},{257,385},{3... | collective-permute-start | bytes 786440 | tf_op jit(solution)/shard_map/ppermute | solution.py:29
  186.5 0.1 copy.27
  186.6 0.7 convert_element_type.44
  187.3 1.9 collective-permute-start
  189.2 17.0 %collective-permute-done.2 = bf16[1,64,2048]{2,1,0:T(8,128)(2,1)S(1)} collective-permute-done((bf16[1,64,2048]{2,1,0:T(8,128)(2,1)S(1)}, bf16[1,64,2048]{2,1,0:T(8,128)(2,1)S(1)}, u32[]{:S(2)}, u32[]{:S(2)}) %collective-permute-start.2) | collective-permute-done | bytes 262176 | tf_op jit(solution)/shard_map/ppermute | solution.py:29
  206.2 13.1 %collective-permute-done = bf16[1,64,2048]{2,1,0:T(8,128)(2,1)S(1)} collective-permute-done((bf16[1,64,2048]{2,1,0:T(8,128)(2,1)S(1)}, bf16[1,64,2048]{2,1,0:T(8,128)(2,1)S(1)}, u32[]{:S(2)}, u32[]{:S(2)}) %collective-permute-start) | collective-permute-done | bytes 262176 | tf_op jit(solution)/shard_map/ppermute | solution.py:22
  219.3 0.8 pad_maximum_fusion
  (10 shorter events, 0.1 us)
Async XLA Ops:
  7.2 3.7 %copy-start = (bf16[1,64,4096]{2,1,0:T(8,128)(2,1)S(1)}, bf16[1,64,4096]{2,1,0:T(8,128)(2,1)}, u32[]{:S(2)}) copy-start(bf16[1,64,4096]{2,1,0:T(8,128)(2,1)} %param.7) | copy-start | bytes 1572868
  7.2 3.7 %copy-start.3 = (bf16[1,4096]{1,0:T(2,128)(2,1)S(1)}, bf16[1,4096]{1,0:T(2,128)(2,1)}, u32[]{:S(2)}) copy-start(bf16[1,4096]{1,0:T(2,128)(2,1)} %param.8) | copy-start | bytes 24580
  7.2 74.5 %all-gather.6.cloned.1.call-start = ((), (), s32[]{:S(2)}) async-start(), calls=%async_computation.1 | async-start | bytes 5406720 | tf_op jit(solution)/shard_map/all_gather | solution.py:121
  7.9 147.9 %all-gather.4.cloned.1.call-start = ((), (), s32[]{:S(2)}) async-start(), calls=%async_computation | async-start | bytes 5406720 | tf_op jit(solution)/shard_map/all_gather | solution.py:130
  19.3 4.9 %copy-start.4 = (s32[1,8]{1,0:T(1,128)S(1)}, s32[1,8]{1,0:T(1,128)}, u32[]{:S(2)}) copy-start(s32[1,8]{1,0:T(1,128)} %param.13) | copy-start | bytes 100
  81.7 5.2 %copy-start.2 = (bf16[1,16,1024]{2,1,0:T(8,128)(2,1)S(1)}, bf16[1,16,1024]{2,1,0:T(8,128)(2,1)}, u32[]{:S(2)}) copy-start(bf16[1,16,1024]{2,1,0:T(8,128)(2,1)} %param.10) | copy-start | bytes 98308
  81.7 74.2 %copy-start.1 = (bf16[1,64,4096]{2,1,0:T(8,128)(2,1)S(1)}, bf16[1,64,4096]{2,1,0:T(8,128)(2,1)}, u32[]{:S(2)}) copy-start(bf16[1,64,4096]{2,1,0:T(8,128)(2,1)} %param.9) | copy-start | bytes 1572868
  167.3 11.5 %collective-permute-start.1 = (bf16[1,64,2048]{2,1,0:T(8,128)(2,1)S(1)}, bf16[1,64,2048]{2,1,0:T(8,128)(2,1)S(1)}, u32[]{:S(2)}, u32[]{:S(2)}) collective-permute-start(bf16[1,64,2048]{2,1,0:T(8,128)(2,1)S(1)} %get-tuple-element.3), channel_id=1, source_target_pairs={{0,32},{32,64},{64,96},{128,160},{160,192},{192,224},{256,288},{28... | collective-permute-start | bytes 786440 | tf_op jit(solution)/shard_map/ppermute | solution.py:23
  178.9 27.3 %collective-permute-start.2 = (bf16[1,64,2048]{2,1,0:T(8,128)(2,1)S(1)}, bf16[1,64,2048]{2,1,0:T(8,128)(2,1)S(1)}, u32[]{:S(2)}, u32[]{:S(2)}) collective-permute-start(bf16[1,64,2048]{2,1,0:T(8,128)(2,1)S(1)} %collective-permute-done.1), channel_id=1, source_target_pairs={{0,128},{128,256},{256,384},{384,0},{1,129},{129,257},{257,385},{3... | collective-permute-start | bytes 786440 | tf_op jit(solution)/shard_map/ppermute | solution.py:29
  187.3 32.0 %collective-permute-start = (bf16[1,64,2048]{2,1,0:T(8,128)(2,1)S(1)}, bf16[1,64,2048]{2,1,0:T(8,128)(2,1)S(1)}, u32[]{:S(2)}, u32[]{:S(2)}) collective-permute-start(bf16[1,64,2048]{2,1,0:T(8,128)(2,1)S(1)} %get-tuple-element.2), channel_id=1, source_target_pairs={{0,32},{32,64},{64,96},{96,128},{128,160},{160,192},{192,224},{224... | collective-permute-start | bytes 786440 | tf_op jit(solution)/shard_map/ppermute | solution.py:22
Sparse Core Ops, SparseCore 0:
  10.1 71.4 all-gather.5
  87.7 68.0 all-gather.3

commit v8 on v7

--- a/solution.py
+++ b/solution.py
@@ -89,7 +89,7 @@
         out_specs=pl.BlockSpec((rows, group_width), lambda g, f: (0, g)),
     )
     return pl.pallas_call(
-        functools.partial(attend_kernel, stack=4),
+        functools.partial(attend_kernel, stack=8),
         grid_spec=grid_spec,
         out_shape=jax.ShapeDtypeStruct((rows, width), jnp.bfloat16),
         compiler_params=pltpu.CompilerParams(vmem_limit_bytes=48 * 1024 * 1024),

time: 227 us -> 233 us (1.026)
  Pallas kernels: 11.4 us -> 16.7 us
    pallas_call x1, Pallas kernels: 11.4 us -> 16.7 us  [attend(): pl.pallas_call(functools.partial(attend_kernel, stack=8), grid_spec=grid_...]
where the time goes in v8:
time: 233 us; the launch traced here: 232 us
  waiting for transfers between devices  162 us (70%)
  Pallas kernels  16.7 us (7%)
  local copies, waits for them, and re-layouts  14.6 us (6%)
  between operations  14.3 us (6%)
  starting transfers between devices  13 us (6%)
  other arithmetic  6.14 us (3%)
  matrix products  5.15 us (2%)
    all_gather x1, waiting for transfers between devices, local(): lax.all_gather(jnp.concatenate([kv_new, cached_kv[0]], axis=0), 'zero', a...  68.1 us
    all_gather x1, waiting for transfers between devices, local(): every_block = lax.all_gather(panel_blocks[0], 'zero', axis=0, tiled=True)  55.5 us
    ppermute x1, waiting for transfers between devices, relay_along(): lax.ppermute(second, axis, [(p + 1 - span, (p + 1) % size) for p in cross...  17 us
    pallas_call x1, Pallas kernels, attend(): pl.pallas_call(functools.partial(attend_kernel, stack=8), grid_spec=grid_...  16.7 us
    ppermute x1, waiting for transfers between devices, relay_along(): lax.ppermute(direct_half, axis, [(p, (p + 1) % size) for p in range(size)])  13.1 us
    gather x3, local copies, waits for them, and re-layouts, local(): jnp.take(normed_grid, row_table, axis=1)  12.4 us
    ppermute x1, waiting for transfers between devices, relay_along(): lax.ppermute(relayed_half, axis, [(p, (p + 1) % size) for p in range(size...  8.14 us
    ppermute x1, starting transfers between devices, relay_along(): lax.ppermute(second, axis, [(p + 1 - span, (p + 1) % size) for p in cross...  7.63 us
  transfers between devices with their start and end apart: 5, of which 5 were waited for; matrix products, arithmetic and copies ran while one was open for 8% of the time, Pallas kernels for 0%

profile of v8, /device:TPU:64, one launch (start us, length us, event | category | flops | bytes accessed | tf_op | source)
XLA Modules:
  0.0 232.2 jit_solution(12703986386689206454)
XLA Ops:
  7.2 0.0 copy-start
  7.2 0.0 copy-start.3
  7.2 0.0 all-gather.6.cloned.1.call-start
  7.2 0.7 all-gather.6.cloned.1.call-update
  7.9 0.0 all-gather.4.cloned.1.call-start
  8.0 0.8 reshape_squeeze.6
  8.7 0.7 compare_and_fusion
  9.4 0.1 copy.22
  9.5 1.1 convert_bitcast_fusion
  10.6 0.2 copy.30
  10.8 0.0 copy-done.3
  10.9 0.0 copy-done
  10.9 0.2 multiply_reduce_fusion
  11.1 0.7 fusion.6
  11.8 2.5 %gather_fusion = bf16[160,64,128]{2,1,0:T(8,128)(2,1)} fusion(bf16[64,32,128]{2,0,1:T(8,128)(2,1)S(1)} %fusion.6, s32[1024]{0:T(1024)S(1)} %pad_clamp_fusion), kind=kCustom, calls=%fused_computation | custom fusion | bytes 5243520 | tf_op jit(solution)/shard_map/jit(_take)/gather | solution.py:122
  14.4 5.0 %copy.24 = bf16[64,160,128]{2,1,0:T(8,128)(2,1)} copy(bf16[64,160,128]{2,0,1:T(8,128)(2,1)} %bitcast.35) | data formatting | bytes 5242880 | tf_op jit(solution)/shard_map/jit(_take)/gather | solution.py:122
  19.3 0.0 copy-start.4
  19.3 4.9 %gather.7 = bf16[64,8,2560]{2,1,0:T(8,128)(2,1)S(1)} reshape(bf16[64,160,128]{2,1,0:T(8,128)(2,1)} %copy.24) | data formatting | bytes 5242880 | tf_op jit(solution)/shard_map/jit(_take)/gather | solution.py:122
  24.3 0.0 copy-done.4
  24.3 0.1 broadcast_bitcast_fusion
  24.4 1.8 select_select_fusion
  26.2 55.5 %all-gather.6.cloned.1.call-done = bf16[1,160,128,128]{3,2,0,1:T(8,128)(2,1)} async-done(((bf16[1,5,128,128]{3,2,0,1:T(8,128)(2,1)}), bf16[1,160,128,128]{3,2,0,1:T(8,128)(2,1)}) %all-gather.6.cloned.1.call-update) | async-done | bytes 5242896 | tf_op jit(solution)/shard_map/all_gather | solution.py:121
  81.7 0.0 copy-start.2
  81.7 0.0 copy-start.1
  81.7 5.1 %fusion.2 = bf16[8,64,128]{2,1,0:T(8,128)(2,1)S(1)} fusion(bf16[8,2560,128]{2,1,0:T(8,128)(2,1)} %bitcast.34, bf16[64,8,2560]{2,1,0:T(8,128)(2,1)} %select_select_fusion), kind=kOutput, calls=%fused_computation.4 | convolution fusion | flops 335609856 | bytes 7995392 | tf_op jit(solution)/shard_map/rpk,pkn->rpn/dot_general | solution.py:123
  86.9 0.0 copy-done.2
  86.9 0.7 pad_maximum_fusion.1
  87.6 0.0 all-gather.4.cloned.1.call-update
  87.6 0.1 add_select_fusion
  87.7 0.1 select_n.57.pos_ref
  87.8 68.1 %all-gather.4.cloned.1.call-done.k_ref.v_ref = bf16[2560,1024]{1,0:T(8,128)(2,1)} async-done(((bf16[80,1024]{1,0:T(8,128)(2,1)}), bf16[2560,1024]{1,0:T(8,128)(2,1)}) %all-gather.4.cloned.1.call-update) | async-done | bytes 5242896 | tf_op jit(solution)/shard_map/all_gather | solution.py:130
  155.8 0.0 copy-done.1
  155.8 16.7 %shard_map.86 = bf16[64,4096]{1,0:T(8,128)(2,1)S(1)} custom-call(s32[1]{0:T(128)} %bitcast.first_ref, s32[1,2560]{1,0:T(1,128)S(1)} %select_n.57.pos_ref, bf16[64,4096]{1,0:T(8,128)(2,1)S(1)} %bitcast.33, bf16[64,4096]{1,0:T(8,128)(2,1)S(1)} %bitcast.31, bf16[2560,1024]{1,0:T(8,128)(2,1)} %all-gather.4.cloned.1.call-done.k_ref.v_ref, ...), custom_call_target="tpu_custom_call" | custom-call | flops 2684354560 | bytes 6815744 | tf_op jit(solution)/shard_map/pallas_call | solution.py:91
  172.6 3.4 %collective-permute-start.1 = (bf16[1,64,2048]{2,1,0:T(8,128)(2,1)S(1)}, bf16[1,64,2048]{2,1,0:T(8,128)(2,1)S(1)}, u32[]{:S(2)}, u32[]{:S(2)}) collective-permute-start(bf16[1,64,2048]{2,1,0:T(8,128)(2,1)S(1)} %get-tuple-element.3), channel_id=1, source_target_pairs={{0,32},{32,64},{64,96},{128,160},{160,192},{192,224},{256,288},{28... | collective-permute-start | bytes 786440 | tf_op jit(solution)/shard_map/ppermute | solution.py:23
  176.0 8.1 %collective-permute-done.1 = bf16[1,64,2048]{2,1,0:T(8,128)(2,1)S(1)} collective-permute-done((bf16[1,64,2048]{2,1,0:T(8,128)(2,1)S(1)}, bf16[1,64,2048]{2,1,0:T(8,128)(2,1)S(1)}, u32[]{:S(2)}, u32[]{:S(2)}) %collective-permute-start.1) | collective-permute-done | bytes 262176 | tf_op jit(solution)/shard_map/ppermute | solution.py:23
  184.1 7.6 %collective-permute-start.2 = (bf16[1,64,2048]{2,1,0:T(8,128)(2,1)S(1)}, bf16[1,64,2048]{2,1,0:T(8,128)(2,1)S(1)}, u32[]{:S(2)}, u32[]{:S(2)}) collective-permute-start(bf16[1,64,2048]{2,1,0:T(8,128)(2,1)S(1)} %collective-permute-done.1), channel_id=1, source_target_pairs={{0,128},{128,256},{256,384},{384,0},{1,129},{129,257},{257,385},{3... | collective-permute-start | bytes 786440 | tf_op jit(solution)/shard_map/ppermute | solution.py:29
  191.8 0.1 copy.27
  191.9 0.7 convert_element_type.44
  192.6 1.9 collective-permute-start
  194.5 17.0 %collective-permute-done.2 = bf16[1,64,2048]{2,1,0:T(8,128)(2,1)S(1)} collective-permute-done((bf16[1,64,2048]{2,1,0:T(8,128)(2,1)S(1)}, bf16[1,64,2048]{2,1,0:T(8,128)(2,1)S(1)}, u32[]{:S(2)}, u32[]{:S(2)}) %collective-permute-start.2) | collective-permute-done | bytes 262176 | tf_op jit(solution)/shard_map/ppermute | solution.py:29
  211.5 13.1 %collective-permute-done = bf16[1,64,2048]{2,1,0:T(8,128)(2,1)S(1)} collective-permute-done((bf16[1,64,2048]{2,1,0:T(8,128)(2,1)S(1)}, bf16[1,64,2048]{2,1,0:T(8,128)(2,1)S(1)}, u32[]{:S(2)}, u32[]{:S(2)}) %collective-permute-start) | collective-permute-done | bytes 262176 | tf_op jit(solution)/shard_map/ppermute | solution.py:22
  224.6 0.8 pad_maximum_fusion
  (10 shorter events, 0.1 us)
Async XLA Ops:
  7.2 3.7 %copy-start = (bf16[1,64,4096]{2,1,0:T(8,128)(2,1)S(1)}, bf16[1,64,4096]{2,1,0:T(8,128)(2,1)}, u32[]{:S(2)}) copy-start(bf16[1,64,4096]{2,1,0:T(8,128)(2,1)} %param.7) | copy-start | bytes 1572868
  7.2 3.7 %copy-start.3 = (bf16[1,4096]{1,0:T(2,128)(2,1)S(1)}, bf16[1,4096]{1,0:T(2,128)(2,1)}, u32[]{:S(2)}) copy-start(bf16[1,4096]{1,0:T(2,128)(2,1)} %param.8) | copy-start | bytes 24580
  7.2 74.5 %all-gather.6.cloned.1.call-start = ((), (), s32[]{:S(2)}) async-start(), calls=%async_computation.1 | async-start | bytes 5406720 | tf_op jit(solution)/shard_map/all_gather | solution.py:121
  7.9 147.9 %all-gather.4.cloned.1.call-start = ((), (), s32[]{:S(2)}) async-start(), calls=%async_computation | async-start | bytes 5406720 | tf_op jit(solution)/shard_map/all_gather | solution.py:130
  19.3 4.9 %copy-start.4 = (s32[1,8]{1,0:T(1,128)S(1)}, s32[1,8]{1,0:T(1,128)}, u32[]{:S(2)}) copy-start(s32[1,8]{1,0:T(1,128)} %param.13) | copy-start | bytes 100
  81.7 5.2 %copy-start.2 = (bf16[1,16,1024]{2,1,0:T(8,128)(2,1)S(1)}, bf16[1,16,1024]{2,1,0:T(8,128)(2,1)}, u32[]{:S(2)}) copy-start(bf16[1,16,1024]{2,1,0:T(8,128)(2,1)} %param.10) | copy-start | bytes 98308
  81.7 74.2 %copy-start.1 = (bf16[1,64,4096]{2,1,0:T(8,128)(2,1)S(1)}, bf16[1,64,4096]{2,1,0:T(8,128)(2,1)}, u32[]{:S(2)}) copy-start(bf16[1,64,4096]{2,1,0:T(8,128)(2,1)} %param.9) | copy-start | bytes 1572868
  172.6 11.5 %collective-permute-start.1 = (bf16[1,64,2048]{2,1,0:T(8,128)(2,1)S(1)}, bf16[1,64,2048]{2,1,0:T(8,128)(2,1)S(1)}, u32[]{:S(2)}, u32[]{:S(2)}) collective-permute-start(bf16[1,64,2048]{2,1,0:T(8,128)(2,1)S(1)} %get-tuple-element.3), channel_id=1, source_target_pairs={{0,32},{32,64},{64,96},{128,160},{160,192},{192,224},{256,288},{28... | collective-permute-start | bytes 786440 | tf_op jit(solution)/shard_map/ppermute | solution.py:23
  184.1 27.3 %collective-permute-start.2 = (bf16[1,64,2048]{2,1,0:T(8,128)(2,1)S(1)}, bf16[1,64,2048]{2,1,0:T(8,128)(2,1)S(1)}, u32[]{:S(2)}, u32[]{:S(2)}) collective-permute-start(bf16[1,64,2048]{2,1,0:T(8,128)(2,1)S(1)} %collective-permute-done.1), channel_id=1, source_target_pairs={{0,128},{128,256},{256,384},{384,0},{1,129},{129,257},{257,385},{3... | collective-permute-start | bytes 786440 | tf_op jit(solution)/shard_map/ppermute | solution.py:29
  192.6 32.0 %collective-permute-start = (bf16[1,64,2048]{2,1,0:T(8,128)(2,1)S(1)}, bf16[1,64,2048]{2,1,0:T(8,128)(2,1)S(1)}, u32[]{:S(2)}, u32[]{:S(2)}) collective-permute-start(bf16[1,64,2048]{2,1,0:T(8,128)(2,1)S(1)} %get-tuple-element.2), channel_id=1, source_target_pairs={{0,32},{32,64},{64,96},{96,128},{128,160},{160,192},{192,224},{224... | collective-permute-start | bytes 786440 | tf_op jit(solution)/shard_map/ppermute | solution.py:22
Sparse Core Ops, SparseCore 0:
  10.1 71.4 all-gather.5
  87.7 68.0 all-gather.3
